TPU v7x, 256 devices: a whole 4x4x8 slice. The times are simulated.
256 devices in a mesh: seq: 64 (over z, y, core), head: 4 (over x).
Axes of the slice: x: 4, y: 4, z: 8, core: 2. Of those that a mesh axis runs over, the one named last changes fastest.
Arguments:
- query: bfloat16 [40960, 2048], P(('seq', 'head')), may hold values from -5 to 5
- key: bfloat16 [40960, 2048], P(('seq', 'head')), may hold values from -5 to 5
- value: bfloat16 [40960, 2048], P(('seq', 'head')), may hold values from -6 to 6
- grad_out: bfloat16 [40960, 2048], P(('seq', 'head')), may hold values from -6 to 6
- rand_blocks: int32 [640, 3], replicated, may hold values from 0 to 639, as said below
Outputs:
- grad_query: bfloat16 [40960, 2048], P(('seq', 'head'))
- grad_key: bfloat16 [40960, 2048], P(('seq', 'head'))
- grad_value: bfloat16 [40960, 2048], P(('seq', 'head'))
Inputs may be any that keep to these rules, and one draw needn't show every extreme that they name: `rand_blocks`: row j lists the 3 random key blocks of query block j. Block b lies on index b // 10 of seq. The blocks of one row lie on 3 different indices. No listed block lies on index 0 or on the index of the query block itself. The query blocks of one index of seq list at most 1 block lying on any one other index.
All inputs are finite; a program needn't handle non-finite values.
Results may differ from a plain program's by a relative error of at most 0.008.
Values may be sent and summed in bfloat16 or wider, within the bound.
No kernel may reach another device: no remote copies, remote signals or barrier semaphores. Data moves between devices by JAX's collectives and lax.ppermute only.
A program may use at most 384 MiB of HBM per device.

v0:
```python
import jax
import jax.numpy as jnp
from jax import lax
from jax.sharding import PartitionSpec as P

HD = 128
BLOCK = 64
G = 2
R = 3


big_negative = -1e30


def broadcast(block, axis, source):
    peers = lax.axis_size(axis)
    block = jnp.where(lax.axis_index(axis) == source, block, jnp.zeros_like(block))
    inner = 8 if peers % 8 == 0 else 1
    if inner > 1 and source == 0:
        outer = peers // inner
        received = [
            lax.ppermute(block, axis, [(0, k * inner)]) for k in range(1, outer)
        ]
        for part in received:
            block = block + part
        received = [
            lax.ppermute(block, axis, [(z * inner, z * inner + k) for z in range(outer)])
            for k in range(1, inner)
        ]
        for part in received:
            block = block + part
        return block
    step = 1
    while step * 2 < peers:
        step *= 2
    while step >= 1:
        pairs = [(i, i + step) for i in range(0, peers, 2 * step) if i + step < peers]
        block = block + lax.ppermute(block, axis, pairs)
        step //= 2
    return block


def reduce_to_first(block, axis):
    peers = lax.axis_size(axis)
    step = 1
    while step < peers:
        radix = 4 if peers % (step * 4) == 0 else 2
        received = [
            lax.ppermute(
                block, axis, [(i + k * step, i) for i in range(0, peers, radix * step)]
            )
            for k in range(1, radix)
        ]
        for part in received:
            block = block + part
        step *= radix
    return block


def extended_2(shard, sides, width):
    for axis, dim in sides:
        peers, length = (lax.axis_size(axis), shard.shape[dim])
        up = [(i, (i + 1) % peers) for i in range(peers - 1)]
        down = [(j, i) for i, j in up]
        last = lax.slice_in_dim(shard, length - width, length, axis=dim)
        leading = lax.slice_in_dim(shard, 0, width, axis=dim)
        before = lax.ppermute(last, axis, up)
        after = lax.ppermute(leading, axis, down)
        shard = jnp.concatenate([before, shard, after], axis=dim)
    return shard


def request_plan(requested, device, per_dev):
    wanted_row = requested[device]
    owners = wanted_row // per_dev
    within = wanted_row % per_dev
    usable = jnp.ones(wanted_row.shape, jnp.bool_)
    positions = jnp.arange(owners.shape[0])
    earlier = (owners[:, None] == owners[None, :]) & (positions[None, :] < positions[:, None])
    slot_rank = jnp.sum(earlier.astype(jnp.int32), axis=1)
    return (owners, within, slot_rank, usable)


def attend_chunk(queries, out_grads, own_pairs, outgoing, global_pairs, extended,
                 chooser, my_slot, my_usable, device, seq_count, capacity, early=False):
    tokens, features = queries.shape
    head_count = features // HD
    per_dev = tokens // BLOCK
    rand_count = per_dev * R
    score_scale = HD ** (-0.5)

    left_pair = extended[:, :BLOCK]
    right_pair = extended[:, -BLOCK:]
    framed = jnp.concatenate([left_pair[:, None], own_pairs, right_pair[:, None]], axis=1)
    window = jnp.stack(
        [framed[:, 0:per_dev], framed[:, 1 : per_dev + 1], framed[:, 2 : per_dev + 2]], axis=2
    )
    global_slots = jnp.broadcast_to(global_pairs[:, None], (2, per_dev, G, BLOCK, features))
    local = jnp.concatenate([window, global_slots], axis=2)
    local_count = 3 + G
    local_keys = local[0].reshape(per_dev, local_count, BLOCK, head_count, HD)
    local_values = local[1].reshape(per_dev, local_count, BLOCK, head_count, HD)
    block_index = device * per_dev + jnp.arange(per_dev)
    glob_index = jnp.arange(G)
    intersections = jnp.abs(glob_index[None, :] - block_index[:, None]) <= 1
    live_local = jnp.concatenate(
        [
            (block_index >= 1)[:, None],
            jnp.ones((per_dev, 1), jnp.bool_),
            (block_index <= seq_count * per_dev - 2)[:, None],
            jnp.logical_not(intersections),
        ],
        axis=1,
    )
    query_blocks = queries.reshape(per_dev, BLOCK, head_count, HD)
    dout_blocks = out_grads.reshape(per_dev, BLOCK, head_count, HD)
    scores_local = (
        jnp.einsum("bxhd,bkyhd->bhxky", query_blocks, local_keys, preferred_element_type=jnp.float32)
        * score_scale
    )
    scores_local = jnp.where(live_local[:, None, None, :, None], scores_local, big_negative)
    grads_local = jnp.einsum(
        "bxhd,bkyhd->bhxky", dout_blocks, local_values, preferred_element_type=jnp.float32
    )
    max_local = jnp.max(scores_local, axis=(3, 4), keepdims=True)

    if early:
        outgoing, scores_local, grads_local, max_local = lax.optimization_barrier(
            (outgoing, scores_local, grads_local, max_local)
        )
    incoming = lax.all_to_all(outgoing, "seq", split_axis=0, concat_axis=0, tiled=True)
    fetched = incoming[my_slot]
    randoms = fetched.reshape(per_dev, R, 2, BLOCK, features)
    rand_keys = randoms[:, :, 0].reshape(per_dev, R, BLOCK, head_count, HD)
    rand_values = randoms[:, :, 1].reshape(per_dev, R, BLOCK, head_count, HD)
    scores_rand = (
        jnp.einsum("bxhd,bkyhd->bhxky", query_blocks, rand_keys, preferred_element_type=jnp.float32)
        * score_scale
    )
    grads_rand = jnp.einsum(
        "bxhd,bkyhd->bhxky", dout_blocks, rand_values, preferred_element_type=jnp.float32
    )
    row_max = jnp.maximum(max_local, jnp.max(scores_rand, axis=(3, 4), keepdims=True))
    weights_local = jnp.exp(scores_local - row_max)
    weights_rand = jnp.exp(scores_rand - row_max)
    row_total = jnp.sum(weights_local, axis=(3, 4), keepdims=True) + jnp.sum(
        weights_rand, axis=(3, 4), keepdims=True
    )
    probs_local = weights_local / row_total
    probs_rand = weights_rand / row_total
    row_dot = jnp.sum(probs_local * grads_local, axis=(3, 4), keepdims=True) + jnp.sum(
        probs_rand * grads_rand, axis=(3, 4), keepdims=True
    )
    dscores_rand = (probs_rand * (grads_rand - row_dot)).astype(jnp.bfloat16)
    low_rand = probs_rand.astype(jnp.bfloat16)
    key_rand = (
        jnp.einsum(
            "bhxky,bxhd->bkyhd", dscores_rand, query_blocks, preferred_element_type=jnp.float32
        )
        * score_scale
    )
    value_rand = jnp.einsum(
        "bhxky,bxhd->bkyhd", low_rand, dout_blocks, preferred_element_type=jnp.float32
    )
    rand_terms = (
        jnp.stack([key_rand, value_rand])
        .reshape(2, rand_count, BLOCK, features)
        .transpose(1, 0, 2, 3)
        .astype(jnp.bfloat16)
    )
    dscores_local = (probs_local * (grads_local - row_dot)).astype(jnp.bfloat16)
    low_local = probs_local.astype(jnp.bfloat16)
    key_global = (
        jnp.einsum(
            "bhxky,bxhd->kyhd",
            dscores_local[:, :, :, 3:],
            query_blocks,
            preferred_element_type=jnp.float32,
        )
        * score_scale
    )
    value_global = jnp.einsum(
        "bhxky,bxhd->kyhd", low_local[:, :, :, 3:], dout_blocks, preferred_element_type=jnp.float32
    )
    halves = jnp.stack([key_global, value_global]).reshape(2, G * BLOCK * features)
    is_even = (device % 2) == 0
    partner = [(i, i ^ 1) for i in range(seq_count)]
    handed = lax.ppermute(jnp.where(is_even, halves[1], halves[0]), "seq", partner)
    kept = jnp.where(is_even, halves[0], halves[1]) + handed
    target = jnp.where(my_usable, my_slot, seq_count * capacity)
    placer = (target[:, None] == jnp.arange(seq_count * capacity)[None, :]).astype(jnp.bfloat16)
    outgoing_back = jnp.einsum(
        "js,jkxf->skxf", placer, rand_terms, preferred_element_type=jnp.float32
    ).astype(jnp.bfloat16)
    outgoing_back = outgoing_back.at[0].set(kept.reshape(2, BLOCK, features).astype(jnp.bfloat16))
    arrived = lax.all_to_all(outgoing_back, "seq", split_axis=0, concat_axis=0, tiled=True)
    firsts = arrived.reshape(seq_count, capacity, G * BLOCK * features)[:, 0].astype(jnp.float32)
    firsts = firsts.reshape(seq_count // 2, 2, G * BLOCK * features)
    everywhere = jnp.sum(firsts, axis=0).reshape(2, G, BLOCK, features)

    query_grads = (
        jnp.einsum(
            "bhxky,bkyhd->bxhd", dscores_local, local_keys, preferred_element_type=jnp.float32
        )
        + jnp.einsum(
            "bhxky,bkyhd->bxhd", dscores_rand, rand_keys, preferred_element_type=jnp.float32
        )
    ) * score_scale
    key_terms = (
        jnp.einsum(
            "bhxky,bxhd->bkyhd",
            dscores_local[:, :, :, :3],
            query_blocks,
            preferred_element_type=jnp.float32,
        )
        * score_scale
    )
    value_terms = jnp.einsum(
        "bhxky,bxhd->bkyhd", low_local[:, :, :, :3], dout_blocks, preferred_element_type=jnp.float32
    )
    pair_terms = jnp.stack([key_terms, value_terms]).reshape(2, per_dev, 3, BLOCK, features)
    framed_sum = jnp.pad(pair_terms[:, :, 0], ((0, 0), (0, 2), (0, 0), (0, 0)))
    framed_sum = framed_sum + jnp.pad(pair_terms[:, :, 1], ((0, 0), (1, 1), (0, 0), (0, 0)))
    framed_sum = framed_sum + jnp.pad(pair_terms[:, :, 2], ((0, 0), (2, 0), (0, 0), (0, 0)))
    totals = framed_sum[:, 1 : per_dev + 1]
    rim_terms = jnp.concatenate([framed_sum[:, 0], framed_sum[:, -1]], axis=1)
    widened = extended_2(rim_terms.astype(jnp.bfloat16), (("seq", 1),), BLOCK).astype(
        rim_terms.dtype
    )
    totals = totals.at[:, 0].add(widened[:, :BLOCK])
    totals = totals.at[:, per_dev - 1].add(widened[:, -BLOCK:])
    padded_global = jnp.pad(everywhere, ((0, 0), (0, per_dev - G), (0, 0), (0, 0))) * (
        device == 0
    ).astype(jnp.float32)
    totals = totals + padded_global
    collected = jnp.einsum(
        "dcb,dcsxf->sbxf",
        chooser.astype(jnp.bfloat16),
        arrived.reshape(seq_count, capacity, 2, BLOCK, features),
        preferred_element_type=jnp.float32,
    )
    totals = totals + collected
    return query_grads.reshape(tokens, features), totals, everywhere


def on_device(query, key, value, grad_out, rand_blocks):
    kv_stacked = jnp.stack([key, value])
    kv_stacked = lax.all_to_all(kv_stacked, "head", split_axis=2, concat_axis=1, tiled=True)
    keys, values = kv_stacked[0], kv_stacked[1]
    qo_stacked = jnp.stack([query, grad_out])
    qo_stacked = lax.all_to_all(qo_stacked, "head", split_axis=2, concat_axis=1, tiled=True)
    queries, out_grads = qo_stacked[0], qo_stacked[1]
    tokens, features = queries.shape
    head_count = features // HD
    per_dev = tokens // BLOCK
    seq_count = lax.axis_size("seq")
    device = lax.axis_index("seq")
    capacity = (per_dev * R + seq_count - 3) // (seq_count - 2)
    rand_count = per_dev * R
    score_scale = HD ** (-0.5)
    requested = rand_blocks.reshape(seq_count, rand_count)
    owners_all, within_all, rank_all, usable_all = jax.vmap(
        lambda sender: request_plan(requested, sender, per_dev)
    )(jnp.arange(seq_count, dtype=jnp.int32))
    to_me = usable_all & (owners_all == device)
    slot_ids = jnp.arange(capacity)
    block_ids = jnp.arange(per_dev)
    matches = (
        to_me[:, :, None, None]
        & (rank_all[:, :, None, None] == slot_ids[None, None, :, None])
        & (within_all[:, :, None, None] == block_ids[None, None, None, :])
    )
    chooser = jnp.sum(matches.astype(jnp.float32), axis=1)
    my_owners, my_within, my_rank, my_usable = request_plan(requested, device, per_dev)
    my_slot = jnp.clip(my_owners, 0, seq_count - 1) * capacity + my_rank
    own_pairs = jnp.stack([keys, values]).reshape(2, per_dev, BLOCK, features)
    served = jnp.einsum(
        "dcb,sbxf->dcsxf",
        chooser.astype(jnp.bfloat16),
        own_pairs,
        preferred_element_type=jnp.float32,
    ).astype(jnp.bfloat16)
    outgoing = served.reshape(seq_count * capacity, 2, BLOCK, features)
    leading = jnp.stack([keys[: G * BLOCK], values[: G * BLOCK]])
    global_pairs = broadcast(leading, "seq", 0).reshape(2, G, BLOCK, features)
    extended = extended_2(jnp.stack([keys, values]), (("seq", 1),), BLOCK)
    outgoing, global_pairs, extended = lax.optimization_barrier((outgoing, global_pairs, extended))
    chunk_heads = 2 if head_count % 2 == 0 else 1
    chunk_width = chunk_heads * HD
    pieces = []
    for c0 in range(0, features, chunk_width):
        pieces.append(
            attend_chunk(
                queries[:, c0 : c0 + chunk_width],
                out_grads[:, c0 : c0 + chunk_width],
                own_pairs[..., c0 : c0 + chunk_width],
                outgoing[..., c0 : c0 + chunk_width],
                global_pairs[..., c0 : c0 + chunk_width],
                extended[..., c0 : c0 + chunk_width],
                chooser, my_slot, my_usable, device, seq_count, capacity,
                early=bool(pieces),
            )
        )
    query_grads = jnp.concatenate([p[0] for p in pieces], axis=-1)
    totals = jnp.concatenate([p[1] for p in pieces], axis=-1)
    grad_rows = query_grads.reshape(tokens, features).astype(jnp.bfloat16)
    key_rows = totals[0].reshape(tokens, features).astype(jnp.bfloat16)
    value_rows = totals[1].reshape(tokens, features).astype(jnp.bfloat16)
    result = jnp.stack([grad_rows, key_rows, value_rows])
    result = lax.all_to_all(result, "head", split_axis=1, concat_axis=2, tiled=True)
    return (result[0], result[1], result[2])


def solution(mesh):
    in_specs = (
        P(("seq", "head"), None),
        P(("seq", "head"), None),
        P(("seq", "head"), None),
        P(("seq", "head"), None),
        P(),
    )
    out_specs = (P(("seq", "head"), None), P(("seq", "head"), None), P(("seq", "head"), None))
    return jax.shard_map(
        on_device, mesh=mesh, in_specs=in_specs, out_specs=out_specs, check_vma=False
    )
```

profile of v0, /device:TPU:121, one launch (start us, length us, event | category | flops | bytes accessed | tf_op | source)
XLA Modules:
  0.0 661.7 jit_solution(11654563391357423585)
XLA Ops:
  16.7 18.7 %all-to-all-done = bf16[2,160,2048]{1,0,2:T(2,128)(2,1)S(1)} async-done(((bf16[2,160,2048]{1,0,2:T(2,128)(2,1)}), bf16[2,160,2048]{1,0,2:T(2,128)(2,1)S(1)}, u32[]{:S(2)}, u32[]{:S(2)}) %all-to-all-start) | async-done | bytes 1310752 | tf_op jit(solution)/shard_map/all_to_all | solution.py:248
  50.0 6.8 %collective-permute-start.14 = (bf16[2,64,512]{2,1,0:T(8,128)(2,1)S(1)}, bf16[2,64,512]{2,1,0:T(8,128)(2,1)S(1)}, u32[]{:S(2)}, u32[]{:S(2)}) collective-permute-start(bf16[2,64,512]{2,1,0:T(8,128)(2,1)S(1)} %get-tuple-element.137), channel_id=1, source_target_pairs={{0,4},{4,8},{8,12},{12,16},{16,20},{20,24},{24,28},{28,32},{32,36}... | collective-permute-start | bytes 393224 | tf_op jit(solution)/shard_map/ppermute | solution.py:67
  62.7 5.8 collective-permute-done.15
  85.7 11.9 %all-to-all-start.2 = ((bf16[64,2,64,256]{3,2,1,0:T(8,128)(2,1)}), bf16[64,2,64,256]{3,2,1,0:T(8,128)(2,1)}, u32[]{:S(2)}, u32[]{:S(2)}) async-start(bf16[64,2,64,256]{3,2,1,0:T(8,128)(2,1)} %copy.883), calls=%async_computation.2 | async-start | bytes 8388608 | tf_op jit(solution)/shard_map/all_to_all | solution.py:131
  99.9 5.6 copy.990
  154.7 35.9 %all-to-all-done.2 = bf16[64,2,64,256]{3,2,1,0:T(8,128)(2,1)} async-done(((bf16[64,2,64,256]{3,2,1,0:T(8,128)(2,1)}), bf16[64,2,64,256]{3,2,1,0:T(8,128)(2,1)}, u32[]{:S(2)}, u32[]{:S(2)}) %all-to-all-start.2) | async-done | bytes 4194336 | tf_op jit(solution)/shard_map/all_to_all | solution.py:131
  223.8 8.9 %all-to-all-start.3 = ((bf16[64,2,64,256]{3,2,1,0:T(8,128)(2,1)}), bf16[64,2,64,256]{3,2,1,0:T(8,128)(2,1)}, u32[]{:S(2)}, u32[]{:S(2)}) async-start(bf16[64,2,64,256]{3,2,1,0:T(8,128)(2,1)} %copy.905), calls=%async_computation.3 | async-start | bytes 8388608 | tf_op jit(solution)/shard_map/all_to_all | solution.py:131
  256.2 6.6 copy.938
  262.8 63.0 %all-to-all-done.3 = bf16[64,2,64,256]{3,2,1,0:T(8,128)(2,1)} async-done(((bf16[64,2,64,256]{3,2,1,0:T(8,128)(2,1)}), bf16[64,2,64,256]{3,2,1,0:T(8,128)(2,1)}, u32[]{:S(2)}, u32[]{:S(2)}) %all-to-all-start.3) | async-done | bytes 4194336 | tf_op jit(solution)/shard_map/all_to_all | solution.py:131
  325.8 9.2 %all-to-all-start.4 = ((bf16[64,2,64,256]{3,2,1,0:T(8,128)(2,1)}), bf16[64,2,64,256]{3,2,1,0:T(8,128)(2,1)}, u32[]{:S(2)}, u32[]{:S(2)}) async-start(bf16[64,2,64,256]{3,2,1,0:T(8,128)(2,1)} %copy.938), calls=%async_computation.4 | async-start | bytes 8388608 | tf_op jit(solution)/shard_map/all_to_all | solution.py:196
  386.8 6.6 copy.961
  393.4 34.5 %all-to-all-done.4 = bf16[64,2,64,256]{3,2,1,0:T(8,128)(2,1)} async-done(((bf16[64,2,64,256]{3,2,1,0:T(8,128)(2,1)}), bf16[64,2,64,256]{3,2,1,0:T(8,128)(2,1)}, u32[]{:S(2)}, u32[]{:S(2)}) %all-to-all-start.4) | async-done | bytes 4194336 | tf_op jit(solution)/shard_map/all_to_all | solution.py:196
  427.8 9.4 %all-to-all-start.5 = ((bf16[64,2,64,256]{3,2,1,0:T(8,128)(2,1)}), bf16[64,2,64,256]{3,2,1,0:T(8,128)(2,1)}, u32[]{:S(2)}, u32[]{:S(2)}) async-start(bf16[64,2,64,256]{3,2,1,0:T(8,128)(2,1)} %copy.961), calls=%async_computation.5 | async-start | bytes 8388608 | tf_op jit(solution)/shard_map/all_to_all | solution.py:196
  459.6 4.6 collective-permute-start.16
  468.9 58.9 %collective-permute-done.16 = bf16[2,64,256]{2,1,0:T(8,128)(2,1)S(1)} collective-permute-done((bf16[2,64,256]{2,1,0:T(8,128)(2,1)S(1)}, bf16[2,64,256]{2,1,0:T(8,128)(2,1)S(1)}, u32[]{:S(2)}, u32[]{:S(2)}) %collective-permute-start.16) | collective-permute-done | bytes 65568 | tf_op jit(solution)/shard_map/ppermute | solution.py:67
  559.7 4.9 collective-permute-start.19
  568.9 4.8 collective-permute-done.20
  576.7 9.9 %reshape.675 = f32[32,2,32768]{2,1,0:T(2,128)} reshape(bf16[64,2,64,256]{3,2,1,0:T(8,128)(2,1)} %all-to-all-done.4) | data formatting | bytes 12582912 | tf_op jit(solution)/shard_map/convert_element_type | solution.py:197
  586.6 6.1 reduce_sum.131
  592.9 5.4 bitcast_add_fusion.1
  598.4 10.2 %reshape.676 = f32[32,2,32768]{2,1,0:T(2,128)} reshape(bf16[64,2,64,256]{3,2,1,0:T(8,128)(2,1)} %all-to-all-done.5) | data formatting | bytes 12582912 | tf_op jit(solution)/shard_map/convert_element_type | solution.py:197
  608.5 6.8 %reduce_sum.132 = f32[2,32768]{1,0:T(2,128)} reduce(f32[32,2,32768]{2,1,0:T(2,128)} %reshape.676, f32[]{:T(128)} %constant.208.clone.1), dimensions={0}, to_apply=%region_16.17 | reduce | flops 2031616 | bytes 8650756 | tf_op jit(solution)/shard_map/reduce_sum | solution.py:199
  616.5 4.7 bitcast_add_fusion
  624.6 31.5 %all_to_all.65 = bf16[3,640,512]{2,0,1:T(4,128)(2,1)S(1)} all-to-all(bf16[3,640,512]{2,0,1:T(4,128)(2,1)S(1)} %copy.966), channel_id=1, replica_groups=mesh['seq'=64,'head'=4] {'head'}, dimensions={1} | all-to-all | bytes 3932160 | tf_op jit(solution)/shard_map/all_to_all | solution.py:310
  (364 shorter events, 288.5 us)
Async XLA Ops:
  5.9 29.6 %all-to-all-start = ((bf16[2,160,2048]{1,0,2:T(2,128)(2,1)}), bf16[2,160,2048]{1,0,2:T(2,128)(2,1)S(1)}, u32[]{:S(2)}, u32[]{:S(2)}) async-start(bf16[2,160,2048]{1,0,2:T(2,128)(2,1)} %copy.863), calls=%async_computation | async-start | bytes 4194304 | tf_op jit(solution)/shard_map/all_to_all | solution.py:248
  35.4 50.3 %all-to-all-start.1 = ((bf16[2,160,2048]{1,0,2:T(2,128)(2,1)}), bf16[2,160,2048]{1,0,2:T(2,128)(2,1)}, u32[]{:S(2)}, u32[]{:S(2)}) async-start(bf16[2,160,2048]{1,0,2:T(2,128)(2,1)} %copy.878), calls=%async_computation.1 | async-start | bytes 4194304 | tf_op jit(solution)/shard_map/all_to_all | solution.py:251
  46.8 10.0 %collective-permute-start.3 = (bf16[2,128,512]{2,1,0:T(8,128)(2,1)S(1)}, bf16[2,128,512]{2,1,0:T(8,128)(2,1)S(1)}, u32[]{:S(2)}, u32[]{:S(2)}) collective-permute-start(bf16[2,128,512]{2,1,0:T(8,128)(2,1)S(1)} %maximum_select_fusion), channel_id=1, source_target_pairs={{0,128},{1,129},{2,130},{3,131}} | collective-permute-start | bytes 786440 | tf_op jit(solution)/shard_map/ppermute | solution.py:22
  47.5 11.2 %collective-permute-start.4 = (bf16[2,128,512]{2,1,0:T(8,128)(2,1)S(1)}, bf16[2,128,512]{2,1,0:T(8,128)(2,1)S(1)}, u32[]{:S(2)}, u32[]{:S(2)}) collective-permute-start(bf16[2,128,512]{2,1,0:T(8,128)(2,1)S(1)} %maximum_select_fusion), channel_id=1, source_target_pairs={{0,160},{1,161},{2,162},{3,163}} | collective-permute-start | bytes 786440 | tf_op jit(solution)/shard_map/ppermute | solution.py:22
  48.2 10.5 %collective-permute-start.5 = (bf16[2,128,512]{2,1,0:T(8,128)(2,1)S(1)}, bf16[2,128,512]{2,1,0:T(8,128)(2,1)S(1)}, u32[]{:S(2)}, u32[]{:S(2)}) collective-permute-start(bf16[2,128,512]{2,1,0:T(8,128)(2,1)S(1)} %maximum_select_fusion), channel_id=1, source_target_pairs={{0,192},{1,193},{2,194},{3,195}} | collective-permute-start | bytes 786440 | tf_op jit(solution)/shard_map/ppermute | solution.py:22
  48.9 9.8 %collective-permute-start.6 = (bf16[2,128,512]{2,1,0:T(8,128)(2,1)S(1)}, bf16[2,128,512]{2,1,0:T(8,128)(2,1)S(1)}, u32[]{:S(2)}, u32[]{:S(2)}) collective-permute-start(bf16[2,128,512]{2,1,0:T(8,128)(2,1)S(1)} %maximum_select_fusion), channel_id=1, source_target_pairs={{0,224},{1,225},{2,226},{3,227}} | collective-permute-start | bytes 786440 | tf_op jit(solution)/shard_map/ppermute | solution.py:22
  50.0 11.4 %collective-permute-start.14 = (bf16[2,64,512]{2,1,0:T(8,128)(2,1)S(1)}, bf16[2,64,512]{2,1,0:T(8,128)(2,1)S(1)}, u32[]{:S(2)}, u32[]{:S(2)}) collective-permute-start(bf16[2,64,512]{2,1,0:T(8,128)(2,1)S(1)} %get-tuple-element.137), channel_id=1, source_target_pairs={{0,4},{4,8},{8,12},{12,16},{16,20},{20,24},{24,28},{28,32},{32,36}... | collective-permute-start | bytes 393224 | tf_op jit(solution)/shard_map/ppermute | solution.py:67
  56.8 11.7 %collective-permute-start.15 = (bf16[2,64,512]{2,1,0:T(8,128)(2,1)S(1)}, bf16[2,64,512]{2,1,0:T(8,128)(2,1)S(1)}, u32[]{:S(2)}, u32[]{:S(2)}) collective-permute-start(bf16[2,64,512]{2,1,0:T(8,128)(2,1)S(1)} %get-tuple-element.138), channel_id=1, source_target_pairs={{4,0},{8,4},{12,8},{16,12},{20,16},{24,20},{28,24},{32,28},{36,32}... | collective-permute-start | bytes 393224 | tf_op jit(solution)/shard_map/ppermute | solution.py:68
  58.9 10.3 %collective-permute-start.10 = (bf16[2,128,512]{2,1,0:T(8,128)(2,1)S(1)}, bf16[2,128,512]{2,1,0:T(8,128)(2,1)S(1)}, u32[]{:S(2)}, u32[]{:S(2)}) collective-permute-start(bf16[2,128,512]{2,1,0:T(8,128)(2,1)S(1)} %add_add_fusion.1), channel_id=1, source_target_pairs={{0,16},{32,48},{64,80},{96,112},{128,144},{160,176},{192,208},{224... | collective-permute-start | bytes 786440 | tf_op jit(solution)/shard_map/ppermute | solution.py:27
  59.6 10.3 %collective-permute-start.11 = (bf16[2,128,512]{2,1,0:T(8,128)(2,1)S(1)}, bf16[2,128,512]{2,1,0:T(8,128)(2,1)S(1)}, u32[]{:S(2)}, u32[]{:S(2)}) collective-permute-start(bf16[2,128,512]{2,1,0:T(8,128)(2,1)S(1)} %add_add_fusion.1), channel_id=1, source_target_pairs={{0,20},{32,52},{64,84},{96,116},{128,148},{160,180},{192,212},{224... | collective-permute-start | bytes 786440 | tf_op jit(solution)/shard_map/ppermute | solution.py:27
  60.7 13.5 %collective-permute-start.12 = (bf16[2,128,512]{2,1,0:T(8,128)(2,1)S(1)}, bf16[2,128,512]{2,1,0:T(8,128)(2,1)S(1)}, u32[]{:S(2)}, u32[]{:S(2)}) collective-permute-start(bf16[2,128,512]{2,1,0:T(8,128)(2,1)S(1)} %add_add_fusion.1), channel_id=1, source_target_pairs={{0,24},{32,56},{64,88},{96,120},{128,152},{160,184},{192,216},{224... | collective-permute-start | bytes 786440 | tf_op jit(solution)/shard_map/ppermute | solution.py:27
  61.4 16.7 %collective-permute-start.13 = (bf16[2,128,512]{2,1,0:T(8,128)(2,1)S(1)}, bf16[2,128,512]{2,1,0:T(8,128)(2,1)S(1)}, u32[]{:S(2)}, u32[]{:S(2)}) collective-permute-start(bf16[2,128,512]{2,1,0:T(8,128)(2,1)S(1)} %add_add_fusion.1), channel_id=1, source_target_pairs={{0,28},{32,60},{64,92},{96,124},{128,156},{160,188},{192,220},{224... | collective-permute-start | bytes 786440 | tf_op jit(solution)/shard_map/ppermute | solution.py:27
  68.5 9.6 %collective-permute-start.7 = (bf16[2,128,512]{2,1,0:T(8,128)(2,1)S(1)}, bf16[2,128,512]{2,1,0:T(8,128)(2,1)S(1)}, u32[]{:S(2)}, u32[]{:S(2)}) collective-permute-start(bf16[2,128,512]{2,1,0:T(8,128)(2,1)S(1)} %add_add_fusion.1), channel_id=1, source_target_pairs={{0,4},{32,36},{64,68},{96,100},{128,132},{160,164},{192,196},{224,... | collective-permute-start | bytes 786440 | tf_op jit(solution)/shard_map/ppermute | solution.py:27
  69.2 8.9 %collective-permute-start.8 = (bf16[2,128,512]{2,1,0:T(8,128)(2,1)S(1)}, bf16[2,128,512]{2,1,0:T(8,128)(2,1)S(1)}, u32[]{:S(2)}, u32[]{:S(2)}) collective-permute-start(bf16[2,128,512]{2,1,0:T(8,128)(2,1)S(1)} %add_add_fusion.1), channel_id=1, source_target_pairs={{0,8},{32,40},{64,72},{96,104},{128,136},{160,168},{192,200},{224,... | collective-permute-start | bytes 786440 | tf_op jit(solution)/shard_map/ppermute | solution.py:27
  85.7 104.8 %all-to-all-start.2 = ((bf16[64,2,64,256]{3,2,1,0:T(8,128)(2,1)}), bf16[64,2,64,256]{3,2,1,0:T(8,128)(2,1)}, u32[]{:S(2)}, u32[]{:S(2)}) async-start(bf16[64,2,64,256]{3,2,1,0:T(8,128)(2,1)} %copy.883), calls=%async_computation.2 | async-start | bytes 8388608 | tf_op jit(solution)/shard_map/all_to_all | solution.py:131
  223.8 102.0 %all-to-all-start.3 = ((bf16[64,2,64,256]{3,2,1,0:T(8,128)(2,1)}), bf16[64,2,64,256]{3,2,1,0:T(8,128)(2,1)}, u32[]{:S(2)}, u32[]{:S(2)}) async-start(bf16[64,2,64,256]{3,2,1,0:T(8,128)(2,1)} %copy.905), calls=%async_computation.3 | async-start | bytes 8388608 | tf_op jit(solution)/shard_map/all_to_all | solution.py:131
  235.8 15.4 %collective-permute-start.18 = (f32[32768]{0:T(1024)S(1)}, f32[32768]{0:T(1024)}, u32[]{:S(2)}, u32[]{:S(2)}) collective-permute-start(f32[32768]{0:T(1024)S(1)} %bitcast.424), channel_id=1, source_target_pairs={{0,4},{4,0},{8,12},{12,8},{16,20},{20,16},{24,28},{28,24},{32,36},... | collective-permute-start | bytes 393224 | tf_op jit(solution)/shard_map/ppermute | solution.py:188
  325.8 102.1 %all-to-all-start.4 = ((bf16[64,2,64,256]{3,2,1,0:T(8,128)(2,1)}), bf16[64,2,64,256]{3,2,1,0:T(8,128)(2,1)}, u32[]{:S(2)}, u32[]{:S(2)}) async-start(bf16[64,2,64,256]{3,2,1,0:T(8,128)(2,1)} %copy.938), calls=%async_computation.4 | async-start | bytes 8388608 | tf_op jit(solution)/shard_map/all_to_all | solution.py:196
  363.0 19.8 %collective-permute-start.21 = (f32[32768]{0:T(1024)S(1)}, f32[32768]{0:T(1024)S(1)}, u32[]{:S(2)}, u32[]{:S(2)}) collective-permute-start(f32[32768]{0:T(1024)S(1)} %bitcast.423), channel_id=1, source_target_pairs={{0,4},{4,0},{8,12},{12,8},{16,20},{20,16},{24,28},{28,24},{32,36},... | collective-permute-start | bytes 393224 | tf_op jit(solution)/shard_map/ppermute | solution.py:188
  427.8 170.5 %all-to-all-start.5 = ((bf16[64,2,64,256]{3,2,1,0:T(8,128)(2,1)}), bf16[64,2,64,256]{3,2,1,0:T(8,128)(2,1)}, u32[]{:S(2)}, u32[]{:S(2)}) async-start(bf16[64,2,64,256]{3,2,1,0:T(8,128)(2,1)} %copy.961), calls=%async_computation.5 | async-start | bytes 8388608 | tf_op jit(solution)/shard_map/all_to_all | solution.py:196
  459.6 68.2 %collective-permute-start.16 = (bf16[2,64,256]{2,1,0:T(8,128)(2,1)S(1)}, bf16[2,64,256]{2,1,0:T(8,128)(2,1)S(1)}, u32[]{:S(2)}, u32[]{:S(2)}) collective-permute-start(bf16[2,64,256]{2,1,0:T(8,128)(2,1)S(1)} %get-tuple-element.145), channel_id=1, source_target_pairs={{0,4},{4,8},{8,12},{12,16},{16,20},{20,24},{24,28},{28,32},{32,36}... | collective-permute-start | bytes 196616 | tf_op jit(solution)/shard_map/ppermute | solution.py:67
  464.2 66.5 %collective-permute-start.17 = (bf16[2,64,256]{2,1,0:T(8,128)(2,1)S(1)}, bf16[2,64,256]{2,1,0:T(8,128)(2,1)S(1)}, u32[]{:S(2)}, u32[]{:S(2)}) collective-permute-start(bf16[2,64,256]{2,1,0:T(8,128)(2,1)S(1)} %get-tuple-element.146), channel_id=1, source_target_pairs={{4,0},{8,4},{12,8},{16,12},{20,16},{24,20},{28,24},{32,28},{36,32}... | collective-permute-start | bytes 196616 | tf_op jit(solution)/shard_map/ppermute | solution.py:68
  559.7 9.1 %collective-permute-start.19 = (bf16[2,64,256]{2,1,0:T(8,128)(2,1)S(1)}, bf16[2,64,256]{2,1,0:T(8,128)(2,1)S(1)}, u32[]{:S(2)}, u32[]{:S(2)}) collective-permute-start(bf16[2,64,256]{2,1,0:T(8,128)(2,1)S(1)} %get-tuple-element.147), channel_id=1, source_target_pairs={{0,4},{4,8},{8,12},{12,16},{16,20},{20,24},{24,28},{28,32},{32,36}... | collective-permute-start | bytes 196616 | tf_op jit(solution)/shard_map/ppermute | solution.py:67
  564.6 9.0 %collective-permute-start.20 = (bf16[2,64,256]{2,1,0:T(8,128)(2,1)S(1)}, bf16[2,64,256]{2,1,0:T(8,128)(2,1)S(1)}, u32[]{:S(2)}, u32[]{:S(2)}) collective-permute-start(bf16[2,64,256]{2,1,0:T(8,128)(2,1)S(1)} %get-tuple-element.148), channel_id=1, source_target_pairs={{4,0},{8,4},{12,8},{16,12},{20,16},{24,20},{28,24},{32,28},{36,32}... | collective-permute-start | bytes 196616 | tf_op jit(solution)/shard_map/ppermute | solution.py:68
  (55 other events, 240.3 us)
where the time goes:
time: 673 us; the launch traced here: 662 us
  local copies, waits for them, and re-layouts  229 us (34%)
  waiting for transfers between devices  228 us (34%)
  starting transfers between devices  81.2 us (12%)
  other arithmetic  44.8 us (7%)
  matrix products  44.6 us (7%)
  blocking collectives  31.5 us (5%)
    all_to_all x2, waiting for transfers between devices, attend_chunk(): lax.all_to_all(outgoing, 'seq', split_axis=0, concat_axis=0, tiled=True)  98.8 us
    ppermute x3, waiting for transfers between devices, extended_2(): before = lax.ppermute(last, axis, up)  58.9 us
    all_to_all x2, waiting for transfers between devices, attend_chunk(): lax.all_to_all(outgoing_back, 'seq', split_axis=0, concat_axis=0, tiled=T...  34.5 us
    all_to_all x1, blocking collectives, on_device(): lax.all_to_all(result, 'head', split_axis=1, concat_axis=2, tiled=True)  31.5 us
    another operation x9, local copies, waits for them, and re-layouts, attend_chunk(): jnp.stack([key_terms, value_terms]).reshape(2, per_dev, 3, BLOCK, features)  24.1 us
    scatter x4, local copies, waits for them, and re-layouts, attend_chunk(): outgoing_back.at[0]  21.1 us
    all_to_all x2, starting transfers between devices, attend_chunk(): lax.all_to_all(outgoing, 'seq', split_axis=0, concat_axis=0, tiled=True)  20.8 us
    convert_element_type x2, local copies, waits for them, and re-layouts, attend_chunk(): arrived.reshape(seq_count, capacity, G * BLOCK * features)[:, 0]  20.1 us
  transfers between devices with their start and end apart: 28, of which 9 were waited for; matrix products, arithmetic and copies ran while one was open for 36% of the time, Pallas kernels for 0%

commit v1 on v0

--- a/solution.py
+++ b/solution.py
@@ -224,11 +224,6 @@
     framed_sum = framed_sum + jnp.pad(pair_terms[:, :, 2], ((0, 0), (2, 0), (0, 0), (0, 0)))
     totals = framed_sum[:, 1 : per_dev + 1]
     rim_terms = jnp.concatenate([framed_sum[:, 0], framed_sum[:, -1]], axis=1)
-    widened = extended_2(rim_terms.astype(jnp.bfloat16), (("seq", 1),), BLOCK).astype(
-        rim_terms.dtype
-    )
-    totals = totals.at[:, 0].add(widened[:, :BLOCK])
-    totals = totals.at[:, per_dev - 1].add(widened[:, -BLOCK:])
     padded_global = jnp.pad(everywhere, ((0, 0), (0, per_dev - G), (0, 0), (0, 0))) * (
         device == 0
     ).astype(jnp.float32)
@@ -240,7 +235,7 @@
         preferred_element_type=jnp.float32,
     )
     totals = totals + collected
-    return query_grads.reshape(tokens, features), totals, everywhere
+    return query_grads.reshape(tokens, features), totals, rim_terms
 
 
 def on_device(query, key, value, grad_out, rand_blocks):
@@ -303,6 +298,13 @@
         )
     query_grads = jnp.concatenate([p[0] for p in pieces], axis=-1)
     totals = jnp.concatenate([p[1] for p in pieces], axis=-1)
+    rim_terms = jnp.concatenate([p[2] for p in pieces], axis=-1)
+    rim_terms, totals = lax.optimization_barrier((rim_terms, totals))
+    widened = extended_2(rim_terms.astype(jnp.bfloat16), (("seq", 1),), BLOCK).astype(
+        rim_terms.dtype
+    )
+    totals = totals.at[:, 0].add(widened[:, :BLOCK])
+    totals = totals.at[:, per_dev - 1].add(widened[:, -BLOCK:])
     grad_rows = query_grads.reshape(tokens, features).astype(jnp.bfloat16)
     key_rows = totals[0].reshape(tokens, features).astype(jnp.bfloat16)
     value_rows = totals[1].reshape(tokens, features).astype(jnp.bfloat16)

time: 673 us -> 646 us (0.960)
  the two profiles are of different devices: /device:TPU:121 before, /device:TPU:8 now
where the time goes in v1:
time: 646 us; the launch traced here: 633 us
  local copies, waits for them, and re-layouts  242 us (37%)
  waiting for transfers between devices  200 us (31%)
  starting transfers between devices  58.7 us (9%)
  other arithmetic  49.8 us (8%)
  matrix products  43.1 us (7%)
  blocking collectives  36.5 us (6%)
    all_to_all x2, waiting for transfers between devices, attend_chunk(): lax.all_to_all(outgoing, 'seq', split_axis=0, concat_axis=0, tiled=True)  105 us
    all_to_all x2, waiting for transfers between devices, attend_chunk(): lax.all_to_all(outgoing_back, 'seq', split_axis=0, concat_axis=0, tiled=T...  61.6 us
    all_to_all x1, blocking collectives, on_device(): lax.all_to_all(result, 'head', split_axis=1, concat_axis=2, tiled=True)  36.5 us
    another operation x10, local copies, waits for them, and re-layouts, attend_chunk(): jnp.stack([key_terms, value_terms]).reshape(2, per_dev, 3, BLOCK, features)  26.2 us
    unnamed x127, local copies, waits for them, and re-layouts  25.7 us
    scatter x4, local copies, waits for them, and re-layouts, attend_chunk(): outgoing_back.at[0]  21 us
    convert_element_type x2, local copies, waits for them, and re-layouts, attend_chunk(): arrived.reshape(seq_count, capacity, G * BLOCK * features)[:, 0]  20.1 us
    all_to_all x1, waiting for transfers between devices, on_device(): lax.all_to_all(kv_stacked, 'head', split_axis=2, concat_axis=1, tiled=True)  19.6 us
  transfers between devices with their start and end apart: 26, of which 6 were waited for; matrix products, arithmetic and copies ran while one was open for 36% of the time, Pallas kernels for 0%

profile of v1, /device:TPU:8, one launch (start us, length us, event | category | flops | bytes accessed | tf_op | source)
XLA Modules:
  0.0 633.3 jit_solution(2932385483085524702)
XLA Ops:
  17.0 19.6 %all-to-all-done = bf16[2,160,2048]{1,0,2:T(2,128)(2,1)S(1)} async-done(((bf16[2,160,2048]{1,0,2:T(2,128)(2,1)}), bf16[2,160,2048]{1,0,2:T(2,128)(2,1)S(1)}, u32[]{:S(2)}, u32[]{:S(2)}) %all-to-all-start) | async-done | bytes 1310752 | tf_op jit(solution)/shard_map/all_to_all | solution.py:243
  36.6 4.5 all-to-all-start.1
  66.5 14.7 %collective-permute-done.8 = bf16[2,128,512]{2,1,0:T(8,128)(2,1)S(1)} collective-permute-done((bf16[2,128,512]{2,1,0:T(8,128)(2,1)S(1)}, bf16[2,128,512]{2,1,0:T(8,128)(2,1)S(1)}, u32[]{:S(2)}, u32[]{:S(2)}) %collective-permute-start.8) | collective-permute-done | bytes 262176 | tf_op jit(solution)/shard_map/ppermute | solution.py:27
  84.3 4.5 copy.899
  88.7 9.8 %all-to-all-start.2 = ((bf16[64,2,64,256]{3,2,1,0:T(8,128)(2,1)}), bf16[64,2,64,256]{3,2,1,0:T(8,128)(2,1)}, u32[]{:S(2)}, u32[]{:S(2)}) async-start(bf16[64,2,64,256]{3,2,1,0:T(8,128)(2,1)} %copy.899), calls=%async_computation.2 | async-start | bytes 8388608 | tf_op jit(solution)/shard_map/all_to_all | solution.py:131
  101.5 5.6 copy.1008
  156.5 38.0 %all-to-all-done.2 = bf16[64,2,64,256]{3,2,1,0:T(8,128)(2,1)} async-done(((bf16[64,2,64,256]{3,2,1,0:T(8,128)(2,1)}), bf16[64,2,64,256]{3,2,1,0:T(8,128)(2,1)}, u32[]{:S(2)}, u32[]{:S(2)}) %all-to-all-start.2) | async-done | bytes 4194336 | tf_op jit(solution)/shard_map/all_to_all | solution.py:131
  227.9 5.8 all-to-all-start.3
  256.9 6.5 %copy.958 = bf16[64,2,64,256]{3,2,1,0:T(8,128)(2,1)} copy(bf16[64,2,64,256]{3,0,2,1:T(8,128)(2,1)} %scatter.6) | data formatting | bytes 8388608 | tf_op jit(solution)/shard_map/scatter | solution.py:195
  263.4 66.5 %all-to-all-done.3 = bf16[64,2,64,256]{3,2,1,0:T(8,128)(2,1)} async-done(((bf16[64,2,64,256]{3,2,1,0:T(8,128)(2,1)}), bf16[64,2,64,256]{3,2,1,0:T(8,128)(2,1)}, u32[]{:S(2)}, u32[]{:S(2)}) %all-to-all-start.3) | async-done | bytes 4194336 | tf_op jit(solution)/shard_map/all_to_all | solution.py:131
  329.9 6.3 all-to-all-start.4
  384.1 6.5 %copy.975 = bf16[64,2,64,256]{3,2,1,0:T(8,128)(2,1)} copy(bf16[64,2,64,256]{3,0,2,1:T(8,128)(2,1)} %scatter.9) | data formatting | bytes 8388608 | tf_op jit(solution)/shard_map/scatter | solution.py:195
  390.7 41.5 %all-to-all-done.4 = bf16[64,2,64,256]{3,2,1,0:T(8,128)(2,1)} async-done(((bf16[64,2,64,256]{3,2,1,0:T(8,128)(2,1)}), bf16[64,2,64,256]{3,2,1,0:T(8,128)(2,1)}, u32[]{:S(2)}, u32[]{:S(2)}) %all-to-all-start.4) | async-done | bytes 4194336 | tf_op jit(solution)/shard_map/all_to_all | solution.py:196
  432.2 6.3 all-to-all-start.5
  489.8 9.9 %reshape.605 = f32[32,2,32768]{2,1,0:T(2,128)} reshape(bf16[64,2,64,256]{3,2,1,0:T(8,128)(2,1)} %all-to-all-done.4) | data formatting | bytes 12582912 | tf_op jit(solution)/shard_map/convert_element_type | solution.py:197
  499.8 6.8 %reduce_sum.131 = f32[2,32768]{1,0:T(2,128)} reduce(f32[32,2,32768]{2,1,0:T(2,128)} %reshape.605, f32[]{:T(128)} %constant.168.clone.1), dimensions={0}, to_apply=%region_15.16 | reduce | flops 2031616 | bytes 8650756 | tf_op jit(solution)/shard_map/reduce_sum | solution.py:199
  509.2 5.2 bitcast_add_fusion
  514.4 20.1 %all-to-all-done.5 = bf16[64,2,64,256]{3,2,1,0:T(8,128)(2,1)} async-done(((bf16[64,2,64,256]{3,2,1,0:T(8,128)(2,1)}), bf16[64,2,64,256]{3,2,1,0:T(8,128)(2,1)}, u32[]{:S(2)}, u32[]{:S(2)}) %all-to-all-start.5) | async-done | bytes 4194336 | tf_op jit(solution)/shard_map/all_to_all | solution.py:196
  534.5 10.1 %reshape.606 = f32[32,2,32768]{2,1,0:T(2,128)} reshape(bf16[64,2,64,256]{3,2,1,0:T(8,128)(2,1)} %all-to-all-done.5) | data formatting | bytes 12582912 | tf_op jit(solution)/shard_map/convert_element_type | solution.py:197
  544.6 6.1 reduce_sum.132
  550.8 4.7 fusion
  570.7 6.6 %scatter-add.6 = f32[2,10,64,512]{3,1,2,0:T(8,128)} dynamic-update-slice(f32[2,10,64,512]{3,1,2,0:T(8,128)} %pad_maximum_fusion, f32[2,1,64,512]{3,1,2,0:T(1,128)S(1)} %copy.981, s32[]{:T(128)} %constant.164.clone.1, s32[]{:T(128)} %constant.164.clone.1, s32[]{:T(128)} %constant.164.clone.1, s32[]{:T(128)} %constant.164.clone.1) | dynamic-update-slice | bytes 524292 | tf_op jit(solution)/shard_map/scatter-add | solution.py:306
  579.3 6.4 %scatter-add.9 = f32[2,10,64,512]{3,1,2,0:T(8,128)} dynamic-update-slice(f32[2,10,64,512]{3,1,2,0:T(8,128)} %scatter-add.6, f32[2,1,64,512]{3,1,2,0:T(1,128)S(1)} %slice_add_fusion, s32[]{:T(128)} %constant.164.clone.1, s32[]{:T(128)} %constant.178.clone.1, s32[]{:T(128)} %constant.164.clone.1, s32[]{:T(128)} %constant.164.clone.1) | dynamic-update-slice | bytes 524292 | tf_op jit(solution)/shard_map/scatter-add | solution.py:307
  591.2 36.5 %all_to_all.65 = bf16[3,640,512]{2,0,1:T(4,128)(2,1)S(1)} all-to-all(bf16[3,640,512]{2,0,1:T(4,128)(2,1)S(1)} %copy.984), channel_id=1, replica_groups=mesh['seq'=64,'head'=4] {'head'}, dimensions={1} | all-to-all | bytes 3932160 | tf_op jit(solution)/shard_map/all_to_all | solution.py:312
  (371 shorter events, 282.1 us)
Async XLA Ops:
  5.8 30.8 %all-to-all-start = ((bf16[2,160,2048]{1,0,2:T(2,128)(2,1)}), bf16[2,160,2048]{1,0,2:T(2,128)(2,1)S(1)}, u32[]{:S(2)}, u32[]{:S(2)}) async-start(bf16[2,160,2048]{1,0,2:T(2,128)(2,1)} %copy.879), calls=%async_computation | async-start | bytes 4194304 | tf_op jit(solution)/shard_map/all_to_all | solution.py:243
  36.6 52.1 %all-to-all-start.1 = ((bf16[2,160,2048]{1,0,2:T(2,128)(2,1)}), bf16[2,160,2048]{1,0,2:T(2,128)(2,1)}, u32[]{:S(2)}, u32[]{:S(2)}) async-start(bf16[2,160,2048]{1,0,2:T(2,128)(2,1)} %copy.894), calls=%async_computation.1 | async-start | bytes 4194304 | tf_op jit(solution)/shard_map/all_to_all | solution.py:246
  47.3 3.9 collective-permute-start.2
  48.0 5.1 collective-permute-start.3
  48.7 8.1 %collective-permute-start.4 = (bf16[2,128,512]{2,1,0:T(8,128)(2,1)S(1)}, bf16[2,128,512]{2,1,0:T(8,128)(2,1)S(1)}, u32[]{:S(2)}, u32[]{:S(2)}) collective-permute-start(bf16[2,128,512]{2,1,0:T(8,128)(2,1)S(1)} %maximum_select_fusion), channel_id=1, source_target_pairs={{0,160},{1,161},{2,162},{3,163}} | collective-permute-start | bytes 786440 | tf_op jit(solution)/shard_map/ppermute | solution.py:22
  49.4 7.4 %collective-permute-start.5 = (bf16[2,128,512]{2,1,0:T(8,128)(2,1)S(1)}, bf16[2,128,512]{2,1,0:T(8,128)(2,1)S(1)}, u32[]{:S(2)}, u32[]{:S(2)}) collective-permute-start(bf16[2,128,512]{2,1,0:T(8,128)(2,1)S(1)} %maximum_select_fusion), channel_id=1, source_target_pairs={{0,192},{1,193},{2,194},{3,195}} | collective-permute-start | bytes 786440 | tf_op jit(solution)/shard_map/ppermute | solution.py:22
  50.1 6.7 %collective-permute-start.6 = (bf16[2,128,512]{2,1,0:T(8,128)(2,1)S(1)}, bf16[2,128,512]{2,1,0:T(8,128)(2,1)S(1)}, u32[]{:S(2)}, u32[]{:S(2)}) collective-permute-start(bf16[2,128,512]{2,1,0:T(8,128)(2,1)S(1)} %maximum_select_fusion), channel_id=1, source_target_pairs={{0,224},{1,225},{2,226},{3,227}} | collective-permute-start | bytes 786440 | tf_op jit(solution)/shard_map/ppermute | solution.py:22
  51.2 8.2 %collective-permute-start.14 = (bf16[2,64,512]{2,1,0:T(8,128)(2,1)S(1)}, bf16[2,64,512]{2,1,0:T(8,128)(2,1)S(1)}, u32[]{:S(2)}, u32[]{:S(2)}) collective-permute-start(bf16[2,64,512]{2,1,0:T(8,128)(2,1)S(1)} %get-tuple-element.117), channel_id=1, source_target_pairs={{0,4},{4,8},{8,12},{12,16},{16,20},{20,24},{24,28},{28,32},{32,36}... | collective-permute-start | bytes 393224 | tf_op jit(solution)/shard_map/ppermute | solution.py:67
  53.1 7.0 %collective-permute-start.15 = (bf16[2,64,512]{2,1,0:T(8,128)(2,1)S(1)}, bf16[2,64,512]{2,1,0:T(8,128)(2,1)S(1)}, u32[]{:S(2)}, u32[]{:S(2)}) collective-permute-start(bf16[2,64,512]{2,1,0:T(8,128)(2,1)S(1)} %get-tuple-element.118), channel_id=1, source_target_pairs={{4,0},{8,4},{12,8},{16,12},{20,16},{24,20},{28,24},{32,28},{36,32}... | collective-permute-start | bytes 393224 | tf_op jit(solution)/shard_map/ppermute | solution.py:68
  57.0 3.9 collective-permute-start.10
  57.6 4.5 collective-permute-start.11
  58.7 7.7 %collective-permute-start.12 = (bf16[2,128,512]{2,1,0:T(8,128)(2,1)S(1)}, bf16[2,128,512]{2,1,0:T(8,128)(2,1)S(1)}, u32[]{:S(2)}, u32[]{:S(2)}) collective-permute-start(bf16[2,128,512]{2,1,0:T(8,128)(2,1)S(1)} %add_add_fusion.1), channel_id=1, source_target_pairs={{0,24},{32,56},{64,88},{96,120},{128,152},{160,184},{192,216},{224... | collective-permute-start | bytes 786440 | tf_op jit(solution)/shard_map/ppermute | solution.py:27
  59.4 7.0 %collective-permute-start.13 = (bf16[2,128,512]{2,1,0:T(8,128)(2,1)S(1)}, bf16[2,128,512]{2,1,0:T(8,128)(2,1)S(1)}, u32[]{:S(2)}, u32[]{:S(2)}) collective-permute-start(bf16[2,128,512]{2,1,0:T(8,128)(2,1)S(1)} %add_add_fusion.1), channel_id=1, source_target_pairs={{0,28},{32,60},{64,92},{96,124},{128,156},{160,188},{192,220},{224... | collective-permute-start | bytes 786440 | tf_op jit(solution)/shard_map/ppermute | solution.py:27
  60.1 6.3 collective-permute-start.7
  60.8 20.3 %collective-permute-start.8 = (bf16[2,128,512]{2,1,0:T(8,128)(2,1)S(1)}, bf16[2,128,512]{2,1,0:T(8,128)(2,1)S(1)}, u32[]{:S(2)}, u32[]{:S(2)}) collective-permute-start(bf16[2,128,512]{2,1,0:T(8,128)(2,1)S(1)} %add_add_fusion.1), channel_id=1, source_target_pairs={{0,8},{32,40},{64,72},{96,104},{128,136},{160,168},{192,200},{224,... | collective-permute-start | bytes 786440 | tf_op jit(solution)/shard_map/ppermute | solution.py:27
  62.1 19.0 %collective-permute-start.9 = (bf16[2,128,512]{2,1,0:T(8,128)(2,1)S(1)}, bf16[2,128,512]{2,1,0:T(8,128)(2,1)S(1)}, u32[]{:S(2)}, u32[]{:S(2)}) collective-permute-start(bf16[2,128,512]{2,1,0:T(8,128)(2,1)S(1)} %add_add_fusion.1), channel_id=1, source_target_pairs={{0,12},{32,44},{64,76},{96,108},{128,140},{160,172},{192,204},{224... | collective-permute-start | bytes 786440 | tf_op jit(solution)/shard_map/ppermute | solution.py:27
  88.7 105.7 %all-to-all-start.2 = ((bf16[64,2,64,256]{3,2,1,0:T(8,128)(2,1)}), bf16[64,2,64,256]{3,2,1,0:T(8,128)(2,1)}, u32[]{:S(2)}, u32[]{:S(2)}) async-start(bf16[64,2,64,256]{3,2,1,0:T(8,128)(2,1)} %copy.899), calls=%async_computation.2 | async-start | bytes 8388608 | tf_op jit(solution)/shard_map/all_to_all | solution.py:131
  227.9 102.0 %all-to-all-start.3 = ((bf16[64,2,64,256]{3,2,1,0:T(8,128)(2,1)}), bf16[64,2,64,256]{3,2,1,0:T(8,128)(2,1)}, u32[]{:S(2)}, u32[]{:S(2)}) async-start(bf16[64,2,64,256]{3,2,1,0:T(8,128)(2,1)} %copy.921), calls=%async_computation.3 | async-start | bytes 8388608 | tf_op jit(solution)/shard_map/all_to_all | solution.py:131
  236.8 15.1 %collective-permute-start.16 = (f32[32768]{0:T(1024)S(1)}, f32[32768]{0:T(1024)}, u32[]{:S(2)}, u32[]{:S(2)}) collective-permute-start(f32[32768]{0:T(1024)S(1)} %bitcast.416), channel_id=1, source_target_pairs={{0,4},{4,0},{8,12},{12,8},{16,20},{20,16},{24,28},{28,24},{32,36},... | collective-permute-start | bytes 393224 | tf_op jit(solution)/shard_map/ppermute | solution.py:188
  329.9 102.3 %all-to-all-start.4 = ((bf16[64,2,64,256]{3,2,1,0:T(8,128)(2,1)}), bf16[64,2,64,256]{3,2,1,0:T(8,128)(2,1)}, u32[]{:S(2)}, u32[]{:S(2)}) async-start(bf16[64,2,64,256]{3,2,1,0:T(8,128)(2,1)} %copy.958), calls=%async_computation.4 | async-start | bytes 8388608 | tf_op jit(solution)/shard_map/all_to_all | solution.py:196
  364.3 15.8 %collective-permute-start.17 = (f32[32768]{0:T(1024)S(1)}, f32[32768]{0:T(1024)S(1)}, u32[]{:S(2)}, u32[]{:S(2)}) collective-permute-start(f32[32768]{0:T(1024)S(1)} %bitcast.415), channel_id=1, source_target_pairs={{0,4},{4,0},{8,12},{12,8},{16,20},{20,16},{24,28},{28,24},{32,36},... | collective-permute-start | bytes 393224 | tf_op jit(solution)/shard_map/ppermute | solution.py:188
  432.2 102.3 %all-to-all-start.5 = ((bf16[64,2,64,256]{3,2,1,0:T(8,128)(2,1)}), bf16[64,2,64,256]{3,2,1,0:T(8,128)(2,1)}, u32[]{:S(2)}, u32[]{:S(2)}) async-start(bf16[64,2,64,256]{3,2,1,0:T(8,128)(2,1)} %copy.975), calls=%async_computation.5 | async-start | bytes 8388608 | tf_op jit(solution)/shard_map/all_to_all | solution.py:196
  559.9 10.4 %collective-permute-start.18 = (bf16[2,64,512]{2,1,0:T(8,128)(2,1)S(1)}, bf16[2,64,512]{2,1,0:T(8,128)(2,1)S(1)}, u32[]{:S(2)}, u32[]{:S(2)}) collective-permute-start(bf16[2,64,512]{2,1,0:T(8,128)(2,1)S(1)} %get-tuple-element.129), channel_id=1, source_target_pairs={{0,4},{4,8},{8,12},{12,16},{16,20},{20,24},{24,28},{28,32},{32,36}... | collective-permute-start | bytes 393224 | tf_op jit(solution)/shard_map/ppermute | solution.py:67
  561.9 8.5 %collective-permute-start.19 = (bf16[2,64,512]{2,1,0:T(8,128)(2,1)S(1)}, bf16[2,64,512]{2,1,0:T(8,128)(2,1)S(1)}, u32[]{:S(2)}, u32[]{:S(2)}) collective-permute-start(bf16[2,64,512]{2,1,0:T(8,128)(2,1)S(1)} %get-tuple-element.130), channel_id=1, source_target_pairs={{4,0},{8,4},{12,8},{16,12},{20,16},{24,20},{28,24},{32,28},{36,32}... | collective-permute-start | bytes 393224 | tf_op jit(solution)/shard_map/ppermute | solution.py:68
  (61 other events, 214.0 us)

commit v2 on v1

--- a/solution.py
+++ b/solution.py
@@ -81,12 +81,10 @@
     return (owners, within, slot_rank, usable)
 
 
-def attend_chunk(queries, out_grads, own_pairs, outgoing, global_pairs, extended,
-                 chooser, my_slot, my_usable, device, seq_count, capacity, early=False):
+def local_chunk(queries, out_grads, own_pairs, global_pairs, extended, device, seq_count):
     tokens, features = queries.shape
     head_count = features // HD
     per_dev = tokens // BLOCK
-    rand_count = per_dev * R
     score_scale = HD ** (-0.5)
 
     left_pair = extended[:, :BLOCK]
@@ -123,12 +121,20 @@
         "bxhd,bkyhd->bhxky", dout_blocks, local_values, preferred_element_type=jnp.float32
     )
     max_local = jnp.max(scores_local, axis=(3, 4), keepdims=True)
-
-    if early:
-        outgoing, scores_local, grads_local, max_local = lax.optimization_barrier(
-            (outgoing, scores_local, grads_local, max_local)
-        )
+    return (local_keys, local_values, query_blocks, dout_blocks, scores_local, grads_local, max_local)
+
+
+def attend_chunk(queries, outgoing, state, chooser, my_slot, my_usable, device, seq_count,
+                 capacity, hold=()):
+    tokens, features = queries.shape
+    head_count = features // HD
+    per_dev = tokens // BLOCK
+    rand_count = per_dev * R
+    score_scale = HD ** (-0.5)
+    local_keys, local_values, query_blocks, dout_blocks, scores_local, grads_local, max_local = state
     incoming = lax.all_to_all(outgoing, "seq", split_axis=0, concat_axis=0, tiled=True)
+    if hold:
+        incoming, hold = lax.optimization_barrier((incoming, hold))
     fetched = incoming[my_slot]
     randoms = fetched.reshape(per_dev, R, 2, BLOCK, features)
     rand_keys = randoms[:, :, 0].reshape(per_dev, R, BLOCK, head_count, HD)
@@ -235,7 +241,7 @@
         preferred_element_type=jnp.float32,
     )
     totals = totals + collected
-    return query_grads.reshape(tokens, features), totals, rim_terms
+    return query_grads.reshape(tokens, features), totals, rim_terms, hold
 
 
 def on_device(query, key, value, grad_out, rand_blocks):
@@ -282,20 +288,31 @@
     outgoing, global_pairs, extended = lax.optimization_barrier((outgoing, global_pairs, extended))
     chunk_heads = 2 if head_count % 2 == 0 else 1
     chunk_width = chunk_heads * HD
+    states = [
+        local_chunk(
+            queries[:, c0 : c0 + chunk_width],
+            out_grads[:, c0 : c0 + chunk_width],
+            own_pairs[..., c0 : c0 + chunk_width],
+            global_pairs[..., c0 : c0 + chunk_width],
+            extended[..., c0 : c0 + chunk_width],
+            device,
+            seq_count,
+        )
+        for c0 in range(0, features, chunk_width)
+    ]
     pieces = []
-    for c0 in range(0, features, chunk_width):
-        pieces.append(
-            attend_chunk(
-                queries[:, c0 : c0 + chunk_width],
-                out_grads[:, c0 : c0 + chunk_width],
-                own_pairs[..., c0 : c0 + chunk_width],
-                outgoing[..., c0 : c0 + chunk_width],
-                global_pairs[..., c0 : c0 + chunk_width],
-                extended[..., c0 : c0 + chunk_width],
-                chooser, my_slot, my_usable, device, seq_count, capacity,
-                early=bool(pieces),
-            )
-        )
+    held = ()
+    for index, c0 in enumerate(range(0, features, chunk_width)):
+        state = states[index] if index == 0 else held[index - 1]
+        piece = attend_chunk(
+            queries[:, c0 : c0 + chunk_width],
+            outgoing[..., c0 : c0 + chunk_width],
+            state, chooser, my_slot, my_usable, device, seq_count, capacity,
+            hold=tuple(states[1:]) if index == 0 else (),
+        )
+        if index == 0:
+            held = piece[3]
+        pieces.append(piece)
     query_grads = jnp.concatenate([p[0] for p in pieces], axis=-1)
     totals = jnp.concatenate([p[1] for p in pieces], axis=-1)
     rim_terms = jnp.concatenate([p[2] for p in pieces], axis=-1)

time: 646 us -> 620 us (0.960)
  local copies, waits for them, and re-layouts: 242 us -> 227 us
    all_to_all x2, waiting for transfers between devices: 105 us -> 81.3 us  [attend_chunk(): lax.all_to_all(outgoing, 'seq', split_axis=0, concat_axis=0, tiled=True)]
    all_to_all x2, waiting for transfers between devices: 61.6 us -> 79.1 us  [attend_chunk(): lax.all_to_all(outgoing_back, 'seq', split_axis=0, concat_axis=0, tiled=T...]
    slice x2 -> x3, local copies, waits for them, and re-layouts: 6.78 us -> 13.5 us  [on_device(): outgoing[..., c0:c0 + chunk_width]]
  transfers between devices with their start and end apart: 26 -> 26, of which waited for: 6 -> 6; matrix products, arithmetic and copies ran while one was open for 36% -> 38% of each run, Pallas kernels for 0% -> 0%
where the time goes in v2:
time: 620 us; the launch traced here: 608 us
  local copies, waits for them, and re-layouts  227 us (37%)
  waiting for transfers between devices  195 us (31%)
  starting transfers between devices  59.2 us (10%)
  other arithmetic  49.5 us (8%)
  matrix products  38.8 us (6%)
  blocking collectives  36.5 us (6%)
    all_to_all x2, waiting for transfers between devices, attend_chunk(): lax.all_to_all(outgoing, 'seq', split_axis=0, concat_axis=0, tiled=True)  81.3 us
    all_to_all x2, waiting for transfers between devices, attend_chunk(): lax.all_to_all(outgoing_back, 'seq', split_axis=0, concat_axis=0, tiled=T...  79.1 us
    all_to_all x1, blocking collectives, on_device(): lax.all_to_all(result, 'head', split_axis=1, concat_axis=2, tiled=True)  36.5 us
    another operation x10, local copies, waits for them, and re-layouts, attend_chunk(): jnp.stack([key_terms, value_terms]).reshape(2, per_dev, 3, BLOCK, features)  25.3 us
    unnamed x127, local copies, waits for them, and re-layouts  24.1 us
    scatter x4, local copies, waits for them, and re-layouts, attend_chunk(): outgoing_back.at[0]  21 us
    convert_element_type x2, local copies, waits for them, and re-layouts, attend_chunk(): arrived.reshape(seq_count, capacity, G * BLOCK * features)[:, 0]  19.9 us
    all_to_all x1, waiting for transfers between devices, on_device(): lax.all_to_all(kv_stacked, 'head', split_axis=2, concat_axis=1, tiled=True)  19.6 us
  transfers between devices with their start and end apart: 26, of which 6 were waited for; matrix products, arithmetic and copies ran while one was open for 38% of the time, Pallas kernels for 0%

profile of v2, /device:TPU:8, one launch (start us, length us, event | category | flops | bytes accessed | tf_op | source)
XLA Modules:
  0.0 608.4 jit_solution(11819733446091387839)
XLA Ops:
  16.9 19.6 %all-to-all-done = bf16[2,160,2048]{1,0,2:T(2,128)(2,1)S(1)} async-done(((bf16[2,160,2048]{1,0,2:T(2,128)(2,1)}), bf16[2,160,2048]{1,0,2:T(2,128)(2,1)S(1)}, u32[]{:S(2)}, u32[]{:S(2)}) %all-to-all-start) | async-done | bytes 1310752 | tf_op jit(solution)/shard_map/all_to_all | solution.py:249
  66.5 14.6 %collective-permute-done.8 = bf16[2,128,512]{2,1,0:T(8,128)(2,1)S(1)} collective-permute-done((bf16[2,128,512]{2,1,0:T(8,128)(2,1)S(1)}, bf16[2,128,512]{2,1,0:T(8,128)(2,1)S(1)}, u32[]{:S(2)}, u32[]{:S(2)}) %collective-permute-start.8) | collective-permute-done | bytes 262176 | tf_op jit(solution)/shard_map/ppermute | solution.py:27
  84.2 4.5 copy.899
  88.7 10.1 %all-to-all-start.2 = ((bf16[64,2,64,256]{3,2,1,0:T(8,128)(2,1)}), bf16[64,2,64,256]{3,2,1,0:T(8,128)(2,1)}, u32[]{:S(2)}, u32[]{:S(2)}) async-start(bf16[64,2,64,256]{3,2,1,0:T(8,128)(2,1)} %copy.899), calls=%async_computation.2 | async-start | bytes 8388608 | tf_op jit(solution)/shard_map/all_to_all | solution.py:135
  102.3 5.6 copy.1008
  143.9 6.7 %copy.921 = bf16[64,2,64,256]{3,2,1,0:T(8,128)(2,1)} copy(bf16[64,2,64,256]{3,0,2,1:T(8,128)(2,1)} %get-tuple-element.80) | data formatting | bytes 8388608 | tf_op jit(solution)/shard_map/slice | solution.py:309
  151.2 43.4 %all-to-all-done.2 = bf16[64,2,64,256]{3,2,1,0:T(8,128)(2,1)} async-done(((bf16[64,2,64,256]{3,2,1,0:T(8,128)(2,1)}), bf16[64,2,64,256]{3,2,1,0:T(8,128)(2,1)}, u32[]{:S(2)}, u32[]{:S(2)}) %all-to-all-start.2) | async-done | bytes 4194336 | tf_op jit(solution)/shard_map/all_to_all | solution.py:135
  194.7 5.7 all-to-all-start.3
  252.2 6.5 %copy.958 = bf16[64,2,64,256]{3,2,1,0:T(8,128)(2,1)} copy(bf16[64,2,64,256]{3,0,2,1:T(8,128)(2,1)} %scatter.6) | data formatting | bytes 8388608 | tf_op jit(solution)/shard_map/scatter | solution.py:201
  258.7 37.9 %all-to-all-done.3 = bf16[64,2,64,256]{3,2,1,0:T(8,128)(2,1)} async-done(((bf16[64,2,64,256]{3,2,1,0:T(8,128)(2,1)}), bf16[64,2,64,256]{3,2,1,0:T(8,128)(2,1)}, u32[]{:S(2)}, u32[]{:S(2)}) %all-to-all-start.3) | async-done | bytes 4194336 | tf_op jit(solution)/shard_map/all_to_all | solution.py:135
  296.6 6.3 %all-to-all-start.4 = ((bf16[64,2,64,256]{3,2,1,0:T(8,128)(2,1)}), bf16[64,2,64,256]{3,2,1,0:T(8,128)(2,1)}, u32[]{:S(2)}, u32[]{:S(2)}) async-start(bf16[64,2,64,256]{3,2,1,0:T(8,128)(2,1)} %copy.958), calls=%async_computation.4 | async-start | bytes 8388608 | tf_op jit(solution)/shard_map/all_to_all | solution.py:202
  344.8 6.6 %copy.975 = bf16[64,2,64,256]{3,2,1,0:T(8,128)(2,1)} copy(bf16[64,2,64,256]{3,0,2,1:T(8,128)(2,1)} %scatter.9) | data formatting | bytes 8388608 | tf_op jit(solution)/shard_map/scatter | solution.py:201
  351.4 47.5 %all-to-all-done.4 = bf16[64,2,64,256]{3,2,1,0:T(8,128)(2,1)} async-done(((bf16[64,2,64,256]{3,2,1,0:T(8,128)(2,1)}), bf16[64,2,64,256]{3,2,1,0:T(8,128)(2,1)}, u32[]{:S(2)}, u32[]{:S(2)}) %all-to-all-start.4) | async-done | bytes 4194336 | tf_op jit(solution)/shard_map/all_to_all | solution.py:202
  398.9 5.9 all-to-all-start.5
  451.1 9.9 %reshape.605 = f32[32,2,32768]{2,1,0:T(2,128)} reshape(bf16[64,2,64,256]{3,2,1,0:T(8,128)(2,1)} %all-to-all-done.4) | data formatting | bytes 12582912 | tf_op jit(solution)/shard_map/convert_element_type | solution.py:203
  461.0 6.8 %reduce_sum.131 = f32[2,32768]{1,0:T(2,128)} reduce(f32[32,2,32768]{2,1,0:T(2,128)} %reshape.605, f32[]{:T(128)} %constant.168.clone.1), dimensions={0}, to_apply=%region_15.16 | reduce | flops 2031616 | bytes 8650756 | tf_op jit(solution)/shard_map/reduce_sum | solution.py:205
  469.5 31.6 %all-to-all-done.5 = bf16[64,2,64,256]{3,2,1,0:T(8,128)(2,1)} async-done(((bf16[64,2,64,256]{3,2,1,0:T(8,128)(2,1)}), bf16[64,2,64,256]{3,2,1,0:T(8,128)(2,1)}, u32[]{:S(2)}, u32[]{:S(2)}) %all-to-all-start.5) | async-done | bytes 4194336 | tf_op jit(solution)/shard_map/all_to_all | solution.py:202
  501.0 10.0 %reshape.606 = f32[32,2,32768]{2,1,0:T(2,128)} reshape(bf16[64,2,64,256]{3,2,1,0:T(8,128)(2,1)} %all-to-all-done.5) | data formatting | bytes 12582912 | tf_op jit(solution)/shard_map/convert_element_type | solution.py:203
  511.1 6.8 %reduce_sum.132 = f32[2,32768]{1,0:T(2,128)} reduce(f32[32,2,32768]{2,1,0:T(2,128)} %reshape.606, f32[]{:T(128)} %constant.168.clone.1), dimensions={0}, to_apply=%region_16.17 | reduce | flops 2031616 | bytes 8650756 | tf_op jit(solution)/shard_map/reduce_sum | solution.py:205
  520.5 4.7 fusion
  527.1 5.2 bitcast_add_fusion
  546.4 6.4 %scatter-add.6 = f32[2,10,64,512]{3,1,2,0:T(8,128)} dynamic-update-slice(f32[2,10,64,512]{3,1,2,0:T(8,128)} %pad_maximum_fusion, f32[2,1,64,512]{3,1,2,0:T(1,128)S(1)} %copy.981, s32[]{:T(128)} %constant.164.clone.1, s32[]{:T(128)} %constant.164.clone.1, s32[]{:T(128)} %constant.164.clone.1, s32[]{:T(128)} %constant.164.clone.1) | dynamic-update-slice | bytes 524292 | tf_op jit(solution)/shard_map/scatter-add | solution.py:323
  554.8 6.4 %scatter-add.9 = f32[2,10,64,512]{3,1,2,0:T(8,128)} dynamic-update-slice(f32[2,10,64,512]{3,1,2,0:T(8,128)} %scatter-add.6, f32[2,1,64,512]{3,1,2,0:T(1,128)S(1)} %slice_add_fusion, s32[]{:T(128)} %constant.164.clone.1, s32[]{:T(128)} %constant.178.clone.1, s32[]{:T(128)} %constant.164.clone.1, s32[]{:T(128)} %constant.164.clone.1) | dynamic-update-slice | bytes 524292 | tf_op jit(solution)/shard_map/scatter-add | solution.py:324
  566.5 36.5 %all_to_all.65 = bf16[3,640,512]{2,0,1:T(4,128)(2,1)S(1)} all-to-all(bf16[3,640,512]{2,0,1:T(4,128)(2,1)S(1)} %copy.984), channel_id=1, replica_groups=mesh['seq'=64,'head'=4] {'head'}, dimensions={1} | all-to-all | bytes 3932160 | tf_op jit(solution)/shard_map/all_to_all | solution.py:329
  (371 shorter events, 260.7 us)
Async XLA Ops:
  5.8 30.8 %all-to-all-start = ((bf16[2,160,2048]{1,0,2:T(2,128)(2,1)}), bf16[2,160,2048]{1,0,2:T(2,128)(2,1)S(1)}, u32[]{:S(2)}, u32[]{:S(2)}) async-start(bf16[2,160,2048]{1,0,2:T(2,128)(2,1)} %copy.879), calls=%async_computation | async-start | bytes 4194304 | tf_op jit(solution)/shard_map/all_to_all | solution.py:249
  36.6 52.1 %all-to-all-start.1 = ((bf16[2,160,2048]{1,0,2:T(2,128)(2,1)}), bf16[2,160,2048]{1,0,2:T(2,128)(2,1)}, u32[]{:S(2)}, u32[]{:S(2)}) async-start(bf16[2,160,2048]{1,0,2:T(2,128)(2,1)} %copy.894), calls=%async_computation.1 | async-start | bytes 4194304 | tf_op jit(solution)/shard_map/all_to_all | solution.py:252
  47.3 3.9 collective-permute-start.2
  48.0 5.1 collective-permute-start.3
  48.7 8.1 %collective-permute-start.4 = (bf16[2,128,512]{2,1,0:T(8,128)(2,1)S(1)}, bf16[2,128,512]{2,1,0:T(8,128)(2,1)S(1)}, u32[]{:S(2)}, u32[]{:S(2)}) collective-permute-start(bf16[2,128,512]{2,1,0:T(8,128)(2,1)S(1)} %maximum_select_fusion), channel_id=1, source_target_pairs={{0,160},{1,161},{2,162},{3,163}} | collective-permute-start | bytes 786440 | tf_op jit(solution)/shard_map/ppermute | solution.py:22
  49.4 7.4 %collective-permute-start.5 = (bf16[2,128,512]{2,1,0:T(8,128)(2,1)S(1)}, bf16[2,128,512]{2,1,0:T(8,128)(2,1)S(1)}, u32[]{:S(2)}, u32[]{:S(2)}) collective-permute-start(bf16[2,128,512]{2,1,0:T(8,128)(2,1)S(1)} %maximum_select_fusion), channel_id=1, source_target_pairs={{0,192},{1,193},{2,194},{3,195}} | collective-permute-start | bytes 786440 | tf_op jit(solution)/shard_map/ppermute | solution.py:22
  50.1 6.7 %collective-permute-start.6 = (bf16[2,128,512]{2,1,0:T(8,128)(2,1)S(1)}, bf16[2,128,512]{2,1,0:T(8,128)(2,1)S(1)}, u32[]{:S(2)}, u32[]{:S(2)}) collective-permute-start(bf16[2,128,512]{2,1,0:T(8,128)(2,1)S(1)} %maximum_select_fusion), channel_id=1, source_target_pairs={{0,224},{1,225},{2,226},{3,227}} | collective-permute-start | bytes 786440 | tf_op jit(solution)/shard_map/ppermute | solution.py:22
  51.2 8.2 %collective-permute-start.14 = (bf16[2,64,512]{2,1,0:T(8,128)(2,1)S(1)}, bf16[2,64,512]{2,1,0:T(8,128)(2,1)S(1)}, u32[]{:S(2)}, u32[]{:S(2)}) collective-permute-start(bf16[2,64,512]{2,1,0:T(8,128)(2,1)S(1)} %get-tuple-element.123), channel_id=1, source_target_pairs={{0,4},{4,8},{8,12},{12,16},{16,20},{20,24},{24,28},{28,32},{32,36}... | collective-permute-start | bytes 393224 | tf_op jit(solution)/shard_map/ppermute | solution.py:67
  53.1 7.0 %collective-permute-start.15 = (bf16[2,64,512]{2,1,0:T(8,128)(2,1)S(1)}, bf16[2,64,512]{2,1,0:T(8,128)(2,1)S(1)}, u32[]{:S(2)}, u32[]{:S(2)}) collective-permute-start(bf16[2,64,512]{2,1,0:T(8,128)(2,1)S(1)} %get-tuple-element.124), channel_id=1, source_target_pairs={{4,0},{8,4},{12,8},{16,12},{20,16},{24,20},{28,24},{32,28},{36,32}... | collective-permute-start | bytes 393224 | tf_op jit(solution)/shard_map/ppermute | solution.py:68
  57.0 3.9 collective-permute-start.10
  57.6 4.5 collective-permute-start.11
  58.7 7.8 %collective-permute-start.12 = (bf16[2,128,512]{2,1,0:T(8,128)(2,1)S(1)}, bf16[2,128,512]{2,1,0:T(8,128)(2,1)S(1)}, u32[]{:S(2)}, u32[]{:S(2)}) collective-permute-start(bf16[2,128,512]{2,1,0:T(8,128)(2,1)S(1)} %add_add_fusion.1), channel_id=1, source_target_pairs={{0,24},{32,56},{64,88},{96,120},{128,152},{160,184},{192,216},{224... | collective-permute-start | bytes 786440 | tf_op jit(solution)/shard_map/ppermute | solution.py:27
  59.4 7.1 %collective-permute-start.13 = (bf16[2,128,512]{2,1,0:T(8,128)(2,1)S(1)}, bf16[2,128,512]{2,1,0:T(8,128)(2,1)S(1)}, u32[]{:S(2)}, u32[]{:S(2)}) collective-permute-start(bf16[2,128,512]{2,1,0:T(8,128)(2,1)S(1)} %add_add_fusion.1), channel_id=1, source_target_pairs={{0,28},{32,60},{64,92},{96,124},{128,156},{160,188},{192,220},{224... | collective-permute-start | bytes 786440 | tf_op jit(solution)/shard_map/ppermute | solution.py:27
  60.1 6.4 %collective-permute-start.7 = (bf16[2,128,512]{2,1,0:T(8,128)(2,1)S(1)}, bf16[2,128,512]{2,1,0:T(8,128)(2,1)S(1)}, u32[]{:S(2)}, u32[]{:S(2)}) collective-permute-start(bf16[2,128,512]{2,1,0:T(8,128)(2,1)S(1)} %add_add_fusion.1), channel_id=1, source_target_pairs={{0,4},{32,36},{64,68},{96,100},{128,132},{160,164},{192,196},{224,... | collective-permute-start | bytes 786440 | tf_op jit(solution)/shard_map/ppermute | solution.py:27
  60.8 20.3 %collective-permute-start.8 = (bf16[2,128,512]{2,1,0:T(8,128)(2,1)S(1)}, bf16[2,128,512]{2,1,0:T(8,128)(2,1)S(1)}, u32[]{:S(2)}, u32[]{:S(2)}) collective-permute-start(bf16[2,128,512]{2,1,0:T(8,128)(2,1)S(1)} %add_add_fusion.1), channel_id=1, source_target_pairs={{0,8},{32,40},{64,72},{96,104},{128,136},{160,168},{192,200},{224,... | collective-permute-start | bytes 786440 | tf_op jit(solution)/shard_map/ppermute | solution.py:27
  62.1 19.0 %collective-permute-start.9 = (bf16[2,128,512]{2,1,0:T(8,128)(2,1)S(1)}, bf16[2,128,512]{2,1,0:T(8,128)(2,1)S(1)}, u32[]{:S(2)}, u32[]{:S(2)}) collective-permute-start(bf16[2,128,512]{2,1,0:T(8,128)(2,1)S(1)} %add_add_fusion.1), channel_id=1, source_target_pairs={{0,12},{32,44},{64,76},{96,108},{128,140},{160,172},{192,204},{224... | collective-permute-start | bytes 786440 | tf_op jit(solution)/shard_map/ppermute | solution.py:27
  88.7 106.0 %all-to-all-start.2 = ((bf16[64,2,64,256]{3,2,1,0:T(8,128)(2,1)}), bf16[64,2,64,256]{3,2,1,0:T(8,128)(2,1)}, u32[]{:S(2)}, u32[]{:S(2)}) async-start(bf16[64,2,64,256]{3,2,1,0:T(8,128)(2,1)} %copy.899), calls=%async_computation.2 | async-start | bytes 8388608 | tf_op jit(solution)/shard_map/all_to_all | solution.py:135
  194.7 101.9 %all-to-all-start.3 = ((bf16[64,2,64,256]{3,2,1,0:T(8,128)(2,1)}), bf16[64,2,64,256]{3,2,1,0:T(8,128)(2,1)}, u32[]{:S(2)}, u32[]{:S(2)}) async-start(bf16[64,2,64,256]{3,2,1,0:T(8,128)(2,1)} %copy.921), calls=%async_computation.3 | async-start | bytes 8388608 | tf_op jit(solution)/shard_map/all_to_all | solution.py:135
  237.8 9.5 %collective-permute-start.16 = (f32[32768]{0:T(1024)}, f32[32768]{0:T(1024)}, u32[]{:S(2)}, u32[]{:S(2)}) collective-permute-start(f32[32768]{0:T(1024)} %bitcast.119), channel_id=1, source_target_pairs={{0,4},{4,0},{8,12},{12,8},{16,20},{20,16},{24,28},{28,24},{32,36},... | collective-permute-start | bytes 393224 | tf_op jit(solution)/shard_map/ppermute | solution.py:194
  296.6 102.3 %all-to-all-start.4 = ((bf16[64,2,64,256]{3,2,1,0:T(8,128)(2,1)}), bf16[64,2,64,256]{3,2,1,0:T(8,128)(2,1)}, u32[]{:S(2)}, u32[]{:S(2)}) async-start(bf16[64,2,64,256]{3,2,1,0:T(8,128)(2,1)} %copy.958), calls=%async_computation.4 | async-start | bytes 8388608 | tf_op jit(solution)/shard_map/all_to_all | solution.py:202
  325.2 15.6 %collective-permute-start.17 = (f32[32768]{0:T(1024)S(1)}, f32[32768]{0:T(1024)S(1)}, u32[]{:S(2)}, u32[]{:S(2)}) collective-permute-start(f32[32768]{0:T(1024)S(1)} %bitcast.415), channel_id=1, source_target_pairs={{0,4},{4,0},{8,12},{12,8},{16,20},{20,16},{24,28},{28,24},{32,36},... | collective-permute-start | bytes 393224 | tf_op jit(solution)/shard_map/ppermute | solution.py:194
  398.9 102.1 %all-to-all-start.5 = ((bf16[64,2,64,256]{3,2,1,0:T(8,128)(2,1)}), bf16[64,2,64,256]{3,2,1,0:T(8,128)(2,1)}, u32[]{:S(2)}, u32[]{:S(2)}) async-start(bf16[64,2,64,256]{3,2,1,0:T(8,128)(2,1)} %copy.975), calls=%async_computation.5 | async-start | bytes 8388608 | tf_op jit(solution)/shard_map/all_to_all | solution.py:202
  534.8 11.3 %collective-permute-start.18 = (bf16[2,64,512]{2,1,0:T(8,128)(2,1)S(1)}, bf16[2,64,512]{2,1,0:T(8,128)(2,1)S(1)}, u32[]{:S(2)}, u32[]{:S(2)}) collective-permute-start(bf16[2,64,512]{2,1,0:T(8,128)(2,1)S(1)} %get-tuple-element.135), channel_id=1, source_target_pairs={{0,4},{4,8},{8,12},{12,16},{16,20},{20,24},{24,28},{28,32},{32,36}... | collective-permute-start | bytes 393224 | tf_op jit(solution)/shard_map/ppermute | solution.py:67
  536.9 9.2 %collective-permute-start.19 = (bf16[2,64,512]{2,1,0:T(8,128)(2,1)S(1)}, bf16[2,64,512]{2,1,0:T(8,128)(2,1)S(1)}, u32[]{:S(2)}, u32[]{:S(2)}) collective-permute-start(bf16[2,64,512]{2,1,0:T(8,128)(2,1)S(1)} %get-tuple-element.136), channel_id=1, source_target_pairs={{4,0},{8,4},{12,8},{16,12},{20,16},{24,20},{28,24},{32,28},{36,32}... | collective-permute-start | bytes 393224 | tf_op jit(solution)/shard_map/ppermute | solution.py:68
  (61 other events, 180.2 us)

commit v3 on v2

--- a/solution.py
+++ b/solution.py
@@ -188,7 +188,7 @@
     value_global = jnp.einsum(
         "bhxky,bxhd->kyhd", low_local[:, :, :, 3:], dout_blocks, preferred_element_type=jnp.float32
     )
-    halves = jnp.stack([key_global, value_global]).reshape(2, G * BLOCK * features)
+    halves = jnp.stack([key_global, value_global]).reshape(2, G, BLOCK, features)
     is_even = (device % 2) == 0
     partner = [(i, i ^ 1) for i in range(seq_count)]
     handed = lax.ppermute(jnp.where(is_even, halves[1], halves[0]), "seq", partner)
@@ -198,11 +198,11 @@
     outgoing_back = jnp.einsum(
         "js,jkxf->skxf", placer, rand_terms, preferred_element_type=jnp.float32
     ).astype(jnp.bfloat16)
-    outgoing_back = outgoing_back.at[0].set(kept.reshape(2, BLOCK, features).astype(jnp.bfloat16))
+    outgoing_back = outgoing_back.at[0].set(kept.astype(jnp.bfloat16))
     arrived = lax.all_to_all(outgoing_back, "seq", split_axis=0, concat_axis=0, tiled=True)
-    firsts = arrived.reshape(seq_count, capacity, G * BLOCK * features)[:, 0].astype(jnp.float32)
-    firsts = firsts.reshape(seq_count // 2, 2, G * BLOCK * features)
-    everywhere = jnp.sum(firsts, axis=0).reshape(2, G, BLOCK, features)
+    firsts = arrived.reshape(seq_count, capacity, 2, BLOCK, features)[:, 0]
+    firsts = firsts.reshape(seq_count // 2, 2, G, BLOCK, features)
+    everywhere = jnp.sum(firsts.astype(jnp.float32), axis=0)
 
     query_grads = (
         jnp.einsum(

time: 620 us -> 604 us (0.974)
  local copies, waits for them, and re-layouts: 227 us -> 200 us
  waiting for transfers between devices: 195 us -> 216 us
  other arithmetic: 49.5 us -> 40.8 us
    convert_element_type x4 -> x0, local copies, waits for them, and re-layouts: 19.9 us -> none  [the longest x2 19.9 us: attend_chunk(): arrived.reshape(seq_count, capacity, G * BLOCK * features)[:, 0]]
    all_to_all x2, waiting for transfers between devices: 79.1 us -> 94.3 us  [attend_chunk(): lax.all_to_all(outgoing_back, 'seq', split_axis=0, concat_axis=0, tiled=T...]
    reduce_sum x2, other arithmetic: 13.6 us -> 6.8 us  [attend_chunk(): everywhere = jnp.sum(firsts.astype(jnp.float32), axis=0)]
    unnamed x127 -> x131, local copies, waits for them, and re-layouts: 24.1 us -> 24.4 us
  transfers between devices with their start and end apart: 26 -> 26, of which waited for: 6 -> 6; matrix products, arithmetic and copies ran while one was open for 38% -> 35% of each run, Pallas kernels for 0% -> 0%
where the time goes in v3:
time: 604 us; the launch traced here: 593 us
  waiting for transfers between devices  216 us (36%)
  local copies, waits for them, and re-layouts  200 us (33%)
  starting transfers between devices  59.5 us (10%)
  other arithmetic  40.8 us (7%)
  matrix products  37.2 us (6%)
  blocking collectives  36.5 us (6%)
    all_to_all x2, waiting for transfers between devices, attend_chunk(): lax.all_to_all(outgoing_back, 'seq', split_axis=0, concat_axis=0, tiled=T...  94.3 us
    all_to_all x2, waiting for transfers between devices, attend_chunk(): lax.all_to_all(outgoing, 'seq', split_axis=0, concat_axis=0, tiled=True)  87.3 us
    all_to_all x1, blocking collectives, on_device(): lax.all_to_all(result, 'head', split_axis=1, concat_axis=2, tiled=True)  36.5 us
    another operation x10, local copies, waits for them, and re-layouts, attend_chunk(): jnp.stack([key_terms, value_terms]).reshape(2, per_dev, 3, BLOCK, features)  24.9 us
    unnamed x131, local copies, waits for them, and re-layouts  24.4 us
    scatter x4, local copies, waits for them, and re-layouts, attend_chunk(): outgoing_back = outgoing_back.at[0].set(kept.astype(jnp.bfloat16))  21 us
    all_to_all x1, waiting for transfers between devices, on_device(): lax.all_to_all(kv_stacked, 'head', split_axis=2, concat_axis=1, tiled=True)  19.7 us
    all_to_all x2, starting transfers between devices, attend_chunk(): lax.all_to_all(outgoing, 'seq', split_axis=0, concat_axis=0, tiled=True)  16.1 us
  transfers between devices with their start and end apart: 26, of which 6 were waited for; matrix products, arithmetic and copies ran while one was open for 35% of the time, Pallas kernels for 0%

profile of v3, /device:TPU:8, one launch (start us, length us, event | category | flops | bytes accessed | tf_op | source)
XLA Modules:
  0.0 592.9 jit_solution(14059557343205755479)
XLA Ops:
  5.8 4.4 all-to-all-start
  16.9 19.7 %all-to-all-done = bf16[2,160,2048]{1,0,2:T(2,128)(2,1)S(1)} async-done(((bf16[2,160,2048]{1,0,2:T(2,128)(2,1)}), bf16[2,160,2048]{1,0,2:T(2,128)(2,1)S(1)}, u32[]{:S(2)}, u32[]{:S(2)}) %all-to-all-start) | async-done | bytes 1310752 | tf_op jit(solution)/shard_map/all_to_all | solution.py:249
  36.6 4.5 all-to-all-start.1
  66.5 14.6 %collective-permute-done.8 = bf16[2,128,512]{2,1,0:T(8,128)(2,1)S(1)} collective-permute-done((bf16[2,128,512]{2,1,0:T(8,128)(2,1)S(1)}, bf16[2,128,512]{2,1,0:T(8,128)(2,1)S(1)}, u32[]{:S(2)}, u32[]{:S(2)}) %collective-permute-start.8) | collective-permute-done | bytes 262176 | tf_op jit(solution)/shard_map/ppermute | solution.py:27
  84.3 4.5 copy.885
  88.8 10.1 %all-to-all-start.2 = ((bf16[64,2,64,256]{3,2,1,0:T(8,128)(2,1)}), bf16[64,2,64,256]{3,2,1,0:T(8,128)(2,1)}, u32[]{:S(2)}, u32[]{:S(2)}) async-start(bf16[64,2,64,256]{3,2,1,0:T(8,128)(2,1)} %copy.885), calls=%async_computation.2 | async-start | bytes 8388608 | tf_op jit(solution)/shard_map/all_to_all | solution.py:135
  101.2 5.6 copy.996
  125.5 4.4 copy.907
  130.5 64.3 %all-to-all-done.2 = bf16[64,2,64,256]{3,2,1,0:T(8,128)(2,1)} async-done(((bf16[64,2,64,256]{3,2,1,0:T(8,128)(2,1)}), bf16[64,2,64,256]{3,2,1,0:T(8,128)(2,1)}, u32[]{:S(2)}, u32[]{:S(2)}) %all-to-all-start.2) | async-done | bytes 4194336 | tf_op jit(solution)/shard_map/all_to_all | solution.py:135
  194.7 6.0 %all-to-all-start.3 = ((bf16[64,2,64,256]{3,2,1,0:T(8,128)(2,1)}), bf16[64,2,64,256]{3,2,1,0:T(8,128)(2,1)}, u32[]{:S(2)}, u32[]{:S(2)}) async-start(bf16[64,2,64,256]{3,2,1,0:T(8,128)(2,1)} %copy.907), calls=%async_computation.3 | async-start | bytes 8388608 | tf_op jit(solution)/shard_map/all_to_all | solution.py:135
  207.9 4.5 reshape_squeeze.28
  226.6 4.1 gather_fusion.1
  267.3 6.5 %copy.944 = bf16[64,2,64,256]{3,2,1,0:T(8,128)(2,1)} copy(bf16[64,2,64,256]{3,0,2,1:T(8,128)(2,1)} %scatter.6) | data formatting | bytes 8388608 | tf_op jit(solution)/shard_map/scatter | solution.py:201
  273.8 23.0 %all-to-all-done.3 = bf16[64,2,64,256]{3,2,1,0:T(8,128)(2,1)} async-done(((bf16[64,2,64,256]{3,2,1,0:T(8,128)(2,1)}), bf16[64,2,64,256]{3,2,1,0:T(8,128)(2,1)}, u32[]{:S(2)}, u32[]{:S(2)}) %all-to-all-start.3) | async-done | bytes 4194336 | tf_op jit(solution)/shard_map/all_to_all | solution.py:135
  296.8 6.3 %all-to-all-start.4 = ((bf16[64,2,64,256]{3,2,1,0:T(8,128)(2,1)}), bf16[64,2,64,256]{3,2,1,0:T(8,128)(2,1)}, u32[]{:S(2)}, u32[]{:S(2)}) async-start(bf16[64,2,64,256]{3,2,1,0:T(8,128)(2,1)} %copy.944), calls=%async_computation.4 | async-start | bytes 8388608 | tf_op jit(solution)/shard_map/all_to_all | solution.py:202
  344.9 6.6 %copy.962 = bf16[64,2,64,256]{3,2,1,0:T(8,128)(2,1)} copy(bf16[64,2,64,256]{3,0,2,1:T(8,128)(2,1)} %scatter.9) | data formatting | bytes 8388608 | tf_op jit(solution)/shard_map/scatter | solution.py:201
  351.5 47.7 %all-to-all-done.4 = bf16[64,2,64,256]{3,2,1,0:T(8,128)(2,1)} async-done(((bf16[64,2,64,256]{3,2,1,0:T(8,128)(2,1)}), bf16[64,2,64,256]{3,2,1,0:T(8,128)(2,1)}, u32[]{:S(2)}, u32[]{:S(2)}) %all-to-all-start.4) | async-done | bytes 4194336 | tf_op jit(solution)/shard_map/all_to_all | solution.py:202
  399.2 6.1 %all-to-all-start.5 = ((bf16[64,2,64,256]{3,2,1,0:T(8,128)(2,1)}), bf16[64,2,64,256]{3,2,1,0:T(8,128)(2,1)}, u32[]{:S(2)}, u32[]{:S(2)}) async-start(bf16[64,2,64,256]{3,2,1,0:T(8,128)(2,1)} %copy.962), calls=%async_computation.5 | async-start | bytes 8388608 | tf_op jit(solution)/shard_map/all_to_all | solution.py:202
  454.9 46.6 %all-to-all-done.5 = bf16[64,2,64,256]{3,2,1,0:T(8,128)(2,1)} async-done(((bf16[64,2,64,256]{3,2,1,0:T(8,128)(2,1)}), bf16[64,2,64,256]{3,2,1,0:T(8,128)(2,1)}, u32[]{:S(2)}, u32[]{:S(2)}) %all-to-all-start.5) | async-done | bytes 4194336 | tf_op jit(solution)/shard_map/all_to_all | solution.py:202
  504.9 4.7 fusion
  511.5 5.4 bitcast_add_fusion
  530.8 6.4 %scatter-add.6 = f32[2,10,64,512]{3,1,2,0:T(8,128)} dynamic-update-slice(f32[2,10,64,512]{3,1,2,0:T(8,128)} %pad_maximum_fusion, f32[2,1,64,512]{3,1,2,0:T(1,128)S(1)} %copy.969, s32[]{:T(128)} %constant.164.clone.1, s32[]{:T(128)} %constant.164.clone.1, s32[]{:T(128)} %constant.164.clone.1, s32[]{:T(128)} %constant.164.clone.1) | dynamic-update-slice | bytes 524292 | tf_op jit(solution)/shard_map/scatter-add | solution.py:323
  539.2 6.4 %scatter-add.9 = f32[2,10,64,512]{3,1,2,0:T(8,128)} dynamic-update-slice(f32[2,10,64,512]{3,1,2,0:T(8,128)} %scatter-add.6, f32[2,1,64,512]{3,1,2,0:T(1,128)S(1)} %slice_add_fusion, s32[]{:T(128)} %constant.164.clone.1, s32[]{:T(128)} %constant.178.clone.1, s32[]{:T(128)} %constant.164.clone.1, s32[]{:T(128)} %constant.164.clone.1) | dynamic-update-slice | bytes 524292 | tf_op jit(solution)/shard_map/scatter-add | solution.py:324
  550.9 36.5 %all_to_all.65 = bf16[3,640,512]{2,0,1:T(4,128)(2,1)S(1)} all-to-all(bf16[3,640,512]{2,0,1:T(4,128)(2,1)S(1)} %copy.972), channel_id=1, replica_groups=mesh['seq'=64,'head'=4] {'head'}, dimensions={1} | all-to-all | bytes 3932160 | tf_op jit(solution)/shard_map/all_to_all | solution.py:329
  (371 shorter events, 241.4 us)
Async XLA Ops:
  5.8 30.8 %all-to-all-start = ((bf16[2,160,2048]{1,0,2:T(2,128)(2,1)}), bf16[2,160,2048]{1,0,2:T(2,128)(2,1)S(1)}, u32[]{:S(2)}, u32[]{:S(2)}) async-start(bf16[2,160,2048]{1,0,2:T(2,128)(2,1)} %copy.865), calls=%async_computation | async-start | bytes 4194304 | tf_op jit(solution)/shard_map/all_to_all | solution.py:249
  36.6 52.2 %all-to-all-start.1 = ((bf16[2,160,2048]{1,0,2:T(2,128)(2,1)}), bf16[2,160,2048]{1,0,2:T(2,128)(2,1)}, u32[]{:S(2)}, u32[]{:S(2)}) async-start(bf16[2,160,2048]{1,0,2:T(2,128)(2,1)} %copy.880), calls=%async_computation.1 | async-start | bytes 4194304 | tf_op jit(solution)/shard_map/all_to_all | solution.py:252
  47.3 3.9 collective-permute-start.2
  48.0 5.1 collective-permute-start.3
  48.7 8.1 %collective-permute-start.4 = (bf16[2,128,512]{2,1,0:T(8,128)(2,1)S(1)}, bf16[2,128,512]{2,1,0:T(8,128)(2,1)S(1)}, u32[]{:S(2)}, u32[]{:S(2)}) collective-permute-start(bf16[2,128,512]{2,1,0:T(8,128)(2,1)S(1)} %maximum_select_fusion), channel_id=1, source_target_pairs={{0,160},{1,161},{2,162},{3,163}} | collective-permute-start | bytes 786440 | tf_op jit(solution)/shard_map/ppermute | solution.py:22
  49.4 7.4 %collective-permute-start.5 = (bf16[2,128,512]{2,1,0:T(8,128)(2,1)S(1)}, bf16[2,128,512]{2,1,0:T(8,128)(2,1)S(1)}, u32[]{:S(2)}, u32[]{:S(2)}) collective-permute-start(bf16[2,128,512]{2,1,0:T(8,128)(2,1)S(1)} %maximum_select_fusion), channel_id=1, source_target_pairs={{0,192},{1,193},{2,194},{3,195}} | collective-permute-start | bytes 786440 | tf_op jit(solution)/shard_map/ppermute | solution.py:22
  50.1 6.7 %collective-permute-start.6 = (bf16[2,128,512]{2,1,0:T(8,128)(2,1)S(1)}, bf16[2,128,512]{2,1,0:T(8,128)(2,1)S(1)}, u32[]{:S(2)}, u32[]{:S(2)}) collective-permute-start(bf16[2,128,512]{2,1,0:T(8,128)(2,1)S(1)} %maximum_select_fusion), channel_id=1, source_target_pairs={{0,224},{1,225},{2,226},{3,227}} | collective-permute-start | bytes 786440 | tf_op jit(solution)/shard_map/ppermute | solution.py:22
  51.2 8.2 %collective-permute-start.14 = (bf16[2,64,512]{2,1,0:T(8,128)(2,1)S(1)}, bf16[2,64,512]{2,1,0:T(8,128)(2,1)S(1)}, u32[]{:S(2)}, u32[]{:S(2)}) collective-permute-start(bf16[2,64,512]{2,1,0:T(8,128)(2,1)S(1)} %get-tuple-element.123), channel_id=1, source_target_pairs={{0,4},{4,8},{8,12},{12,16},{16,20},{20,24},{24,28},{28,32},{32,36}... | collective-permute-start | bytes 393224 | tf_op jit(solution)/shard_map/ppermute | solution.py:67
  53.1 7.0 %collective-permute-start.15 = (bf16[2,64,512]{2,1,0:T(8,128)(2,1)S(1)}, bf16[2,64,512]{2,1,0:T(8,128)(2,1)S(1)}, u32[]{:S(2)}, u32[]{:S(2)}) collective-permute-start(bf16[2,64,512]{2,1,0:T(8,128)(2,1)S(1)} %get-tuple-element.124), channel_id=1, source_target_pairs={{4,0},{8,4},{12,8},{16,12},{20,16},{24,20},{28,24},{32,28},{36,32}... | collective-permute-start | bytes 393224 | tf_op jit(solution)/shard_map/ppermute | solution.py:68
  57.0 3.9 collective-permute-start.10
  57.7 4.5 collective-permute-start.11
  58.8 7.7 %collective-permute-start.12 = (bf16[2,128,512]{2,1,0:T(8,128)(2,1)S(1)}, bf16[2,128,512]{2,1,0:T(8,128)(2,1)S(1)}, u32[]{:S(2)}, u32[]{:S(2)}) collective-permute-start(bf16[2,128,512]{2,1,0:T(8,128)(2,1)S(1)} %add_add_fusion.1), channel_id=1, source_target_pairs={{0,24},{32,56},{64,88},{96,120},{128,152},{160,184},{192,216},{224... | collective-permute-start | bytes 786440 | tf_op jit(solution)/shard_map/ppermute | solution.py:27
  59.5 7.0 %collective-permute-start.13 = (bf16[2,128,512]{2,1,0:T(8,128)(2,1)S(1)}, bf16[2,128,512]{2,1,0:T(8,128)(2,1)S(1)}, u32[]{:S(2)}, u32[]{:S(2)}) collective-permute-start(bf16[2,128,512]{2,1,0:T(8,128)(2,1)S(1)} %add_add_fusion.1), channel_id=1, source_target_pairs={{0,28},{32,60},{64,92},{96,124},{128,156},{160,188},{192,220},{224... | collective-permute-start | bytes 786440 | tf_op jit(solution)/shard_map/ppermute | solution.py:27
  60.1 6.3 %collective-permute-start.7 = (bf16[2,128,512]{2,1,0:T(8,128)(2,1)S(1)}, bf16[2,128,512]{2,1,0:T(8,128)(2,1)S(1)}, u32[]{:S(2)}, u32[]{:S(2)}) collective-permute-start(bf16[2,128,512]{2,1,0:T(8,128)(2,1)S(1)} %add_add_fusion.1), channel_id=1, source_target_pairs={{0,4},{32,36},{64,68},{96,100},{128,132},{160,164},{192,196},{224,... | collective-permute-start | bytes 786440 | tf_op jit(solution)/shard_map/ppermute | solution.py:27
  60.8 20.3 %collective-permute-start.8 = (bf16[2,128,512]{2,1,0:T(8,128)(2,1)S(1)}, bf16[2,128,512]{2,1,0:T(8,128)(2,1)S(1)}, u32[]{:S(2)}, u32[]{:S(2)}) collective-permute-start(bf16[2,128,512]{2,1,0:T(8,128)(2,1)S(1)} %add_add_fusion.1), channel_id=1, source_target_pairs={{0,8},{32,40},{64,72},{96,104},{128,136},{160,168},{192,200},{224,... | collective-permute-start | bytes 786440 | tf_op jit(solution)/shard_map/ppermute | solution.py:27
  62.2 19.0 %collective-permute-start.9 = (bf16[2,128,512]{2,1,0:T(8,128)(2,1)S(1)}, bf16[2,128,512]{2,1,0:T(8,128)(2,1)S(1)}, u32[]{:S(2)}, u32[]{:S(2)}) collective-permute-start(bf16[2,128,512]{2,1,0:T(8,128)(2,1)S(1)} %add_add_fusion.1), channel_id=1, source_target_pairs={{0,12},{32,44},{64,76},{96,108},{128,140},{160,172},{192,204},{224... | collective-permute-start | bytes 786440 | tf_op jit(solution)/shard_map/ppermute | solution.py:27
  88.8 106.0 %all-to-all-start.2 = ((bf16[64,2,64,256]{3,2,1,0:T(8,128)(2,1)}), bf16[64,2,64,256]{3,2,1,0:T(8,128)(2,1)}, u32[]{:S(2)}, u32[]{:S(2)}) async-start(bf16[64,2,64,256]{3,2,1,0:T(8,128)(2,1)} %copy.885), calls=%async_computation.2 | async-start | bytes 8388608 | tf_op jit(solution)/shard_map/all_to_all | solution.py:135
  194.7 102.1 %all-to-all-start.3 = ((bf16[64,2,64,256]{3,2,1,0:T(8,128)(2,1)}), bf16[64,2,64,256]{3,2,1,0:T(8,128)(2,1)}, u32[]{:S(2)}, u32[]{:S(2)}) async-start(bf16[64,2,64,256]{3,2,1,0:T(8,128)(2,1)} %copy.907), calls=%async_computation.3 | async-start | bytes 8388608 | tf_op jit(solution)/shard_map/all_to_all | solution.py:135
  253.0 9.3 %collective-permute-start.16 = (f32[2,64,256]{2,1,0:T(8,128)}, f32[2,64,256]{2,1,0:T(8,128)}, u32[]{:S(2)}, u32[]{:S(2)}) collective-permute-start(f32[2,64,256]{2,1,0:T(8,128)} %bitcast.348), channel_id=1, source_target_pairs={{0,4},{4,0},{8,12},{12,8},{16,20},{20,16},{24,28},{28,24},{32,36},... | collective-permute-start | bytes 393224 | tf_op jit(solution)/shard_map/ppermute | solution.py:194
  296.8 102.4 %all-to-all-start.4 = ((bf16[64,2,64,256]{3,2,1,0:T(8,128)(2,1)}), bf16[64,2,64,256]{3,2,1,0:T(8,128)(2,1)}, u32[]{:S(2)}, u32[]{:S(2)}) async-start(bf16[64,2,64,256]{3,2,1,0:T(8,128)(2,1)} %copy.944), calls=%async_computation.4 | async-start | bytes 8388608 | tf_op jit(solution)/shard_map/all_to_all | solution.py:202
  325.3 15.5 %collective-permute-start.17 = (f32[2,64,256]{2,1,0:T(8,128)S(1)}, f32[2,64,256]{2,1,0:T(8,128)S(1)}, u32[]{:S(2)}, u32[]{:S(2)}) collective-permute-start(f32[2,64,256]{2,1,0:T(8,128)S(1)} %bitcast.425), channel_id=1, source_target_pairs={{0,4},{4,0},{8,12},{12,8},{16,20},{20,16},{24,28},{28,24},{32,36},... | collective-permute-start | bytes 393224 | tf_op jit(solution)/shard_map/ppermute | solution.py:194
  399.2 102.3 %all-to-all-start.5 = ((bf16[64,2,64,256]{3,2,1,0:T(8,128)(2,1)}), bf16[64,2,64,256]{3,2,1,0:T(8,128)(2,1)}, u32[]{:S(2)}, u32[]{:S(2)}) async-start(bf16[64,2,64,256]{3,2,1,0:T(8,128)(2,1)} %copy.962), calls=%async_computation.5 | async-start | bytes 8388608 | tf_op jit(solution)/shard_map/all_to_all | solution.py:202
  519.4 11.1 %collective-permute-start.18 = (bf16[2,64,512]{2,1,0:T(8,128)(2,1)S(1)}, bf16[2,64,512]{2,1,0:T(8,128)(2,1)S(1)}, u32[]{:S(2)}, u32[]{:S(2)}) collective-permute-start(bf16[2,64,512]{2,1,0:T(8,128)(2,1)S(1)} %get-tuple-element.135), channel_id=1, source_target_pairs={{0,4},{4,8},{8,12},{12,16},{16,20},{20,24},{24,28},{28,32},{32,36}... | collective-permute-start | bytes 393224 | tf_op jit(solution)/shard_map/ppermute | solution.py:67
  521.5 9.0 %collective-permute-start.19 = (bf16[2,64,512]{2,1,0:T(8,128)(2,1)S(1)}, bf16[2,64,512]{2,1,0:T(8,128)(2,1)S(1)}, u32[]{:S(2)}, u32[]{:S(2)}) collective-permute-start(bf16[2,64,512]{2,1,0:T(8,128)(2,1)S(1)} %get-tuple-element.136), channel_id=1, source_target_pairs={{4,0},{8,4},{12,8},{16,12},{20,16},{24,20},{28,24},{32,28},{36,32}... | collective-permute-start | bytes 393224 | tf_op jit(solution)/shard_map/ppermute | solution.py:68
  (64 other events, 165.5 us)

commit v4 on v3

--- a/solution.py
+++ b/solution.py
@@ -320,8 +320,15 @@
     widened = extended_2(rim_terms.astype(jnp.bfloat16), (("seq", 1),), BLOCK).astype(
         rim_terms.dtype
     )
-    totals = totals.at[:, 0].add(widened[:, :BLOCK])
-    totals = totals.at[:, per_dev - 1].add(widened[:, -BLOCK:])
+    edges = jnp.concatenate(
+        [
+            widened[:, None, :BLOCK],
+            jnp.zeros((2, per_dev - 2, BLOCK, features), widened.dtype),
+            widened[:, None, -BLOCK:],
+        ],
+        axis=1,
+    )
+    totals = totals + edges
     grad_rows = query_grads.reshape(tokens, features).astype(jnp.bfloat16)
     key_rows = totals[0].reshape(tokens, features).astype(jnp.bfloat16)
     value_rows = totals[1].reshape(tokens, features).astype(jnp.bfloat16)

time: 604 us -> 588 us (0.974)
  local copies, waits for them, and re-layouts: 200 us -> 184 us
    scatter-add x2 -> x0, local copies, waits for them, and re-layouts: 12.7 us -> none  [the longest x1 6.38 us: on_device(): totals = totals.at[:, per_dev - 1].add(widened[:, -BLOCK:])]
  transfers between devices with their start and end apart: 26 -> 26, of which waited for: 6 -> 7; matrix products, arithmetic and copies ran while one was open for 35% -> 36% of each run, Pallas kernels for 0% -> 0%
where the time goes in v4:
time: 588 us; the launch traced here: 577 us
  waiting for transfers between devices  217 us (37%)
  local copies, waits for them, and re-layouts  184 us (31%)
  starting transfers between devices  59.5 us (10%)
  other arithmetic  39.2 us (7%)
  blocking collectives  37.5 us (6%)
  matrix products  37.2 us (6%)
    all_to_all x2, waiting for transfers between devices, attend_chunk(): lax.all_to_all(outgoing_back, 'seq', split_axis=0, concat_axis=0, tiled=T...  94.3 us
    all_to_all x2, waiting for transfers between devices, attend_chunk(): lax.all_to_all(outgoing, 'seq', split_axis=0, concat_axis=0, tiled=True)  87.3 us
    all_to_all x1, blocking collectives, on_device(): lax.all_to_all(result, 'head', split_axis=1, concat_axis=2, tiled=True)  37.5 us
    another operation x10, local copies, waits for them, and re-layouts, attend_chunk(): jnp.stack([key_terms, value_terms]).reshape(2, per_dev, 3, BLOCK, features)  24.9 us
    unnamed x131, local copies, waits for them, and re-layouts  24.3 us
    scatter x4, local copies, waits for them, and re-layouts, attend_chunk(): outgoing_back = outgoing_back.at[0].set(kept.astype(jnp.bfloat16))  21 us
    all_to_all x1, waiting for transfers between devices, on_device(): lax.all_to_all(kv_stacked, 'head', split_axis=2, concat_axis=1, tiled=True)  19.7 us
    all_to_all x2, starting transfers between devices, attend_chunk(): lax.all_to_all(outgoing, 'seq', split_axis=0, concat_axis=0, tiled=True)  16.1 us
  transfers between devices with their start and end apart: 26, of which 7 were waited for; matrix products, arithmetic and copies ran while one was open for 36% of the time, Pallas kernels for 0%

profile of v4, /device:TPU:8, one launch (start us, length us, event | category | flops | bytes accessed | tf_op | source)
XLA Modules:
  0.0 576.8 jit_solution(13030033894889353031)
XLA Ops:
  5.9 4.4 all-to-all-start
  16.9 19.7 %all-to-all-done = bf16[2,160,2048]{1,0,2:T(2,128)(2,1)S(1)} async-done(((bf16[2,160,2048]{1,0,2:T(2,128)(2,1)}), bf16[2,160,2048]{1,0,2:T(2,128)(2,1)S(1)}, u32[]{:S(2)}, u32[]{:S(2)}) %all-to-all-start) | async-done | bytes 1310752 | tf_op jit(solution)/shard_map/all_to_all | solution.py:249
  36.6 4.5 all-to-all-start.1
  66.5 14.6 %collective-permute-done.8 = bf16[2,128,512]{2,1,0:T(8,128)(2,1)S(1)} collective-permute-done((bf16[2,128,512]{2,1,0:T(8,128)(2,1)S(1)}, bf16[2,128,512]{2,1,0:T(8,128)(2,1)S(1)}, u32[]{:S(2)}, u32[]{:S(2)}) %collective-permute-start.8) | collective-permute-done | bytes 262176 | tf_op jit(solution)/shard_map/ppermute | solution.py:27
  84.3 4.5 copy.876
  88.8 10.1 %all-to-all-start.2 = ((bf16[64,2,64,256]{3,2,1,0:T(8,128)(2,1)}), bf16[64,2,64,256]{3,2,1,0:T(8,128)(2,1)}, u32[]{:S(2)}, u32[]{:S(2)}) async-start(bf16[64,2,64,256]{3,2,1,0:T(8,128)(2,1)} %copy.876), calls=%async_computation.2 | async-start | bytes 8388608 | tf_op jit(solution)/shard_map/all_to_all | solution.py:135
  101.2 5.6 copy.986
  125.5 4.4 copy.898
  130.5 64.3 %all-to-all-done.2 = bf16[64,2,64,256]{3,2,1,0:T(8,128)(2,1)} async-done(((bf16[64,2,64,256]{3,2,1,0:T(8,128)(2,1)}), bf16[64,2,64,256]{3,2,1,0:T(8,128)(2,1)}, u32[]{:S(2)}, u32[]{:S(2)}) %all-to-all-start.2) | async-done | bytes 4194336 | tf_op jit(solution)/shard_map/all_to_all | solution.py:135
  194.8 6.0 %all-to-all-start.3 = ((bf16[64,2,64,256]{3,2,1,0:T(8,128)(2,1)}), bf16[64,2,64,256]{3,2,1,0:T(8,128)(2,1)}, u32[]{:S(2)}, u32[]{:S(2)}) async-start(bf16[64,2,64,256]{3,2,1,0:T(8,128)(2,1)} %copy.898), calls=%async_computation.3 | async-start | bytes 8388608 | tf_op jit(solution)/shard_map/all_to_all | solution.py:135
  207.9 4.5 reshape_squeeze.28
  226.7 4.1 gather_fusion.1
  263.4 4.0 scatter.6
  267.3 6.5 %copy.935 = bf16[64,2,64,256]{3,2,1,0:T(8,128)(2,1)} copy(bf16[64,2,64,256]{3,0,2,1:T(8,128)(2,1)} %scatter.6) | data formatting | bytes 8388608 | tf_op jit(solution)/shard_map/scatter | solution.py:201
  273.8 23.0 %all-to-all-done.3 = bf16[64,2,64,256]{3,2,1,0:T(8,128)(2,1)} async-done(((bf16[64,2,64,256]{3,2,1,0:T(8,128)(2,1)}), bf16[64,2,64,256]{3,2,1,0:T(8,128)(2,1)}, u32[]{:S(2)}, u32[]{:S(2)}) %all-to-all-start.3) | async-done | bytes 4194336 | tf_op jit(solution)/shard_map/all_to_all | solution.py:135
  296.8 6.3 %all-to-all-start.4 = ((bf16[64,2,64,256]{3,2,1,0:T(8,128)(2,1)}), bf16[64,2,64,256]{3,2,1,0:T(8,128)(2,1)}, u32[]{:S(2)}, u32[]{:S(2)}) async-start(bf16[64,2,64,256]{3,2,1,0:T(8,128)(2,1)} %copy.935), calls=%async_computation.4 | async-start | bytes 8388608 | tf_op jit(solution)/shard_map/all_to_all | solution.py:202
  344.9 6.6 %copy.953 = bf16[64,2,64,256]{3,2,1,0:T(8,128)(2,1)} copy(bf16[64,2,64,256]{3,0,2,1:T(8,128)(2,1)} %scatter.9) | data formatting | bytes 8388608 | tf_op jit(solution)/shard_map/scatter | solution.py:201
  351.5 47.7 %all-to-all-done.4 = bf16[64,2,64,256]{3,2,1,0:T(8,128)(2,1)} async-done(((bf16[64,2,64,256]{3,2,1,0:T(8,128)(2,1)}), bf16[64,2,64,256]{3,2,1,0:T(8,128)(2,1)}, u32[]{:S(2)}, u32[]{:S(2)}) %all-to-all-start.4) | async-done | bytes 4194336 | tf_op jit(solution)/shard_map/all_to_all | solution.py:202
  399.2 6.1 %all-to-all-start.5 = ((bf16[64,2,64,256]{3,2,1,0:T(8,128)(2,1)}), bf16[64,2,64,256]{3,2,1,0:T(8,128)(2,1)}, u32[]{:S(2)}, u32[]{:S(2)}) async-start(bf16[64,2,64,256]{3,2,1,0:T(8,128)(2,1)} %copy.953), calls=%async_computation.5 | async-start | bytes 8388608 | tf_op jit(solution)/shard_map/all_to_all | solution.py:202
  432.8 4.1 reshape.592
  454.9 46.6 %all-to-all-done.5 = bf16[64,2,64,256]{3,2,1,0:T(8,128)(2,1)} async-done(((bf16[64,2,64,256]{3,2,1,0:T(8,128)(2,1)}), bf16[64,2,64,256]{3,2,1,0:T(8,128)(2,1)}, u32[]{:S(2)}, u32[]{:S(2)}) %all-to-all-start.5) | async-done | bytes 4194336 | tf_op jit(solution)/shard_map/all_to_all | solution.py:202
  504.9 4.7 fusion.1
  511.5 5.4 bitcast_add_fusion
  533.9 37.5 %all_to_all.65 = bf16[3,640,512]{2,0,1:T(4,128)(2,1)S(1)} all-to-all(bf16[3,640,512]{2,0,1:T(4,128)(2,1)S(1)} %copy.962), channel_id=1, replica_groups=mesh['seq'=64,'head'=4] {'head'}, dimensions={1} | all-to-all | bytes 3932160 | tf_op jit(solution)/shard_map/all_to_all | solution.py:336
  (369 shorter events, 229.2 us)
Async XLA Ops:
  5.9 30.8 %all-to-all-start = ((bf16[2,160,2048]{1,0,2:T(2,128)(2,1)}), bf16[2,160,2048]{1,0,2:T(2,128)(2,1)S(1)}, u32[]{:S(2)}, u32[]{:S(2)}) async-start(bf16[2,160,2048]{1,0,2:T(2,128)(2,1)} %copy.856), calls=%async_computation | async-start | bytes 4194304 | tf_op jit(solution)/shard_map/all_to_all | solution.py:249
  36.6 52.2 %all-to-all-start.1 = ((bf16[2,160,2048]{1,0,2:T(2,128)(2,1)}), bf16[2,160,2048]{1,0,2:T(2,128)(2,1)}, u32[]{:S(2)}, u32[]{:S(2)}) async-start(bf16[2,160,2048]{1,0,2:T(2,128)(2,1)} %copy.871), calls=%async_computation.1 | async-start | bytes 4194304 | tf_op jit(solution)/shard_map/all_to_all | solution.py:252
  47.3 3.9 collective-permute-start.2
  48.0 5.1 collective-permute-start.3
  48.7 8.1 %collective-permute-start.4 = (bf16[2,128,512]{2,1,0:T(8,128)(2,1)S(1)}, bf16[2,128,512]{2,1,0:T(8,128)(2,1)S(1)}, u32[]{:S(2)}, u32[]{:S(2)}) collective-permute-start(bf16[2,128,512]{2,1,0:T(8,128)(2,1)S(1)} %maximum_select_fusion), channel_id=1, source_target_pairs={{0,160},{1,161},{2,162},{3,163}} | collective-permute-start | bytes 786440 | tf_op jit(solution)/shard_map/ppermute | solution.py:22
  49.4 7.4 %collective-permute-start.5 = (bf16[2,128,512]{2,1,0:T(8,128)(2,1)S(1)}, bf16[2,128,512]{2,1,0:T(8,128)(2,1)S(1)}, u32[]{:S(2)}, u32[]{:S(2)}) collective-permute-start(bf16[2,128,512]{2,1,0:T(8,128)(2,1)S(1)} %maximum_select_fusion), channel_id=1, source_target_pairs={{0,192},{1,193},{2,194},{3,195}} | collective-permute-start | bytes 786440 | tf_op jit(solution)/shard_map/ppermute | solution.py:22
  50.1 6.7 %collective-permute-start.6 = (bf16[2,128,512]{2,1,0:T(8,128)(2,1)S(1)}, bf16[2,128,512]{2,1,0:T(8,128)(2,1)S(1)}, u32[]{:S(2)}, u32[]{:S(2)}) collective-permute-start(bf16[2,128,512]{2,1,0:T(8,128)(2,1)S(1)} %maximum_select_fusion), channel_id=1, source_target_pairs={{0,224},{1,225},{2,226},{3,227}} | collective-permute-start | bytes 786440 | tf_op jit(solution)/shard_map/ppermute | solution.py:22
  51.2 8.2 %collective-permute-start.14 = (bf16[2,64,512]{2,1,0:T(8,128)(2,1)S(1)}, bf16[2,64,512]{2,1,0:T(8,128)(2,1)S(1)}, u32[]{:S(2)}, u32[]{:S(2)}) collective-permute-start(bf16[2,64,512]{2,1,0:T(8,128)(2,1)S(1)} %get-tuple-element.99), channel_id=1, source_target_pairs={{0,4},{4,8},{8,12},{12,16},{16,20},{20,24},{24,28},{28,32},{32,36}... | collective-permute-start | bytes 393224 | tf_op jit(solution)/shard_map/ppermute | solution.py:67
  53.1 7.0 %collective-permute-start.15 = (bf16[2,64,512]{2,1,0:T(8,128)(2,1)S(1)}, bf16[2,64,512]{2,1,0:T(8,128)(2,1)S(1)}, u32[]{:S(2)}, u32[]{:S(2)}) collective-permute-start(bf16[2,64,512]{2,1,0:T(8,128)(2,1)S(1)} %get-tuple-element.100), channel_id=1, source_target_pairs={{4,0},{8,4},{12,8},{16,12},{20,16},{24,20},{28,24},{32,28},{36,32}... | collective-permute-start | bytes 393224 | tf_op jit(solution)/shard_map/ppermute | solution.py:68
  57.0 3.9 collective-permute-start.10
  57.7 4.5 collective-permute-start.11
  58.8 7.7 %collective-permute-start.12 = (bf16[2,128,512]{2,1,0:T(8,128)(2,1)S(1)}, bf16[2,128,512]{2,1,0:T(8,128)(2,1)S(1)}, u32[]{:S(2)}, u32[]{:S(2)}) collective-permute-start(bf16[2,128,512]{2,1,0:T(8,128)(2,1)S(1)} %add_add_fusion.1), channel_id=1, source_target_pairs={{0,24},{32,56},{64,88},{96,120},{128,152},{160,184},{192,216},{224... | collective-permute-start | bytes 786440 | tf_op jit(solution)/shard_map/ppermute | solution.py:27
  59.5 7.0 %collective-permute-start.13 = (bf16[2,128,512]{2,1,0:T(8,128)(2,1)S(1)}, bf16[2,128,512]{2,1,0:T(8,128)(2,1)S(1)}, u32[]{:S(2)}, u32[]{:S(2)}) collective-permute-start(bf16[2,128,512]{2,1,0:T(8,128)(2,1)S(1)} %add_add_fusion.1), channel_id=1, source_target_pairs={{0,28},{32,60},{64,92},{96,124},{128,156},{160,188},{192,220},{224... | collective-permute-start | bytes 786440 | tf_op jit(solution)/shard_map/ppermute | solution.py:27
  60.2 6.3 %collective-permute-start.7 = (bf16[2,128,512]{2,1,0:T(8,128)(2,1)S(1)}, bf16[2,128,512]{2,1,0:T(8,128)(2,1)S(1)}, u32[]{:S(2)}, u32[]{:S(2)}) collective-permute-start(bf16[2,128,512]{2,1,0:T(8,128)(2,1)S(1)} %add_add_fusion.1), channel_id=1, source_target_pairs={{0,4},{32,36},{64,68},{96,100},{128,132},{160,164},{192,196},{224,... | collective-permute-start | bytes 786440 | tf_op jit(solution)/shard_map/ppermute | solution.py:27
  60.9 20.3 %collective-permute-start.8 = (bf16[2,128,512]{2,1,0:T(8,128)(2,1)S(1)}, bf16[2,128,512]{2,1,0:T(8,128)(2,1)S(1)}, u32[]{:S(2)}, u32[]{:S(2)}) collective-permute-start(bf16[2,128,512]{2,1,0:T(8,128)(2,1)S(1)} %add_add_fusion.1), channel_id=1, source_target_pairs={{0,8},{32,40},{64,72},{96,104},{128,136},{160,168},{192,200},{224,... | collective-permute-start | bytes 786440 | tf_op jit(solution)/shard_map/ppermute | solution.py:27
  62.2 19.0 %collective-permute-start.9 = (bf16[2,128,512]{2,1,0:T(8,128)(2,1)S(1)}, bf16[2,128,512]{2,1,0:T(8,128)(2,1)S(1)}, u32[]{:S(2)}, u32[]{:S(2)}) collective-permute-start(bf16[2,128,512]{2,1,0:T(8,128)(2,1)S(1)} %add_add_fusion.1), channel_id=1, source_target_pairs={{0,12},{32,44},{64,76},{96,108},{128,140},{160,172},{192,204},{224... | collective-permute-start | bytes 786440 | tf_op jit(solution)/shard_map/ppermute | solution.py:27
  88.8 106.0 %all-to-all-start.2 = ((bf16[64,2,64,256]{3,2,1,0:T(8,128)(2,1)}), bf16[64,2,64,256]{3,2,1,0:T(8,128)(2,1)}, u32[]{:S(2)}, u32[]{:S(2)}) async-start(bf16[64,2,64,256]{3,2,1,0:T(8,128)(2,1)} %copy.876), calls=%async_computation.2 | async-start | bytes 8388608 | tf_op jit(solution)/shard_map/all_to_all | solution.py:135
  194.8 102.1 %all-to-all-start.3 = ((bf16[64,2,64,256]{3,2,1,0:T(8,128)(2,1)}), bf16[64,2,64,256]{3,2,1,0:T(8,128)(2,1)}, u32[]{:S(2)}, u32[]{:S(2)}) async-start(bf16[64,2,64,256]{3,2,1,0:T(8,128)(2,1)} %copy.898), calls=%async_computation.3 | async-start | bytes 8388608 | tf_op jit(solution)/shard_map/all_to_all | solution.py:135
  253.0 9.3 %collective-permute-start.16 = (f32[2,64,256]{2,1,0:T(8,128)}, f32[2,64,256]{2,1,0:T(8,128)}, u32[]{:S(2)}, u32[]{:S(2)}) collective-permute-start(f32[2,64,256]{2,1,0:T(8,128)} %bitcast.346), channel_id=1, source_target_pairs={{0,4},{4,0},{8,12},{12,8},{16,20},{20,16},{24,28},{28,24},{32,36},... | collective-permute-start | bytes 393224 | tf_op jit(solution)/shard_map/ppermute | solution.py:194
  296.8 102.3 %all-to-all-start.4 = ((bf16[64,2,64,256]{3,2,1,0:T(8,128)(2,1)}), bf16[64,2,64,256]{3,2,1,0:T(8,128)(2,1)}, u32[]{:S(2)}, u32[]{:S(2)}) async-start(bf16[64,2,64,256]{3,2,1,0:T(8,128)(2,1)} %copy.935), calls=%async_computation.4 | async-start | bytes 8388608 | tf_op jit(solution)/shard_map/all_to_all | solution.py:202
  325.3 15.5 %collective-permute-start.17 = (f32[2,64,256]{2,1,0:T(8,128)S(1)}, f32[2,64,256]{2,1,0:T(8,128)S(1)}, u32[]{:S(2)}, u32[]{:S(2)}) collective-permute-start(f32[2,64,256]{2,1,0:T(8,128)S(1)} %bitcast.423), channel_id=1, source_target_pairs={{0,4},{4,0},{8,12},{12,8},{16,20},{20,16},{24,28},{28,24},{32,36},... | collective-permute-start | bytes 393224 | tf_op jit(solution)/shard_map/ppermute | solution.py:194
  399.2 102.3 %all-to-all-start.5 = ((bf16[64,2,64,256]{3,2,1,0:T(8,128)(2,1)}), bf16[64,2,64,256]{3,2,1,0:T(8,128)(2,1)}, u32[]{:S(2)}, u32[]{:S(2)}) async-start(bf16[64,2,64,256]{3,2,1,0:T(8,128)(2,1)} %copy.953), calls=%async_computation.5 | async-start | bytes 8388608 | tf_op jit(solution)/shard_map/all_to_all | solution.py:202
  519.4 7.4 %collective-permute-start.18 = (bf16[2,64,512]{2,1,0:T(8,128)(2,1)S(1)}, bf16[2,64,512]{2,1,0:T(8,128)(2,1)S(1)}, u32[]{:S(2)}, u32[]{:S(2)}) collective-permute-start(bf16[2,64,512]{2,1,0:T(8,128)(2,1)S(1)} %get-tuple-element.113), channel_id=1, source_target_pairs={{0,4},{4,8},{8,12},{12,16},{16,20},{20,24},{24,28},{28,32},{32,36}... | collective-permute-start | bytes 393224 | tf_op jit(solution)/shard_map/ppermute | solution.py:67
  521.5 6.1 %collective-permute-start.19 = (bf16[2,64,512]{2,1,0:T(8,128)(2,1)S(1)}, bf16[2,64,512]{2,1,0:T(8,128)(2,1)S(1)}, u32[]{:S(2)}, u32[]{:S(2)}) collective-permute-start(bf16[2,64,512]{2,1,0:T(8,128)(2,1)S(1)} %get-tuple-element.114), channel_id=1, source_target_pairs={{4,0},{8,4},{12,8},{16,12},{20,16},{24,20},{28,24},{32,28},{36,32}... | collective-permute-start | bytes 393224 | tf_op jit(solution)/shard_map/ppermute | solution.py:68
  (64 other events, 165.4 us)

commit v5 on v4

--- a/solution.py
+++ b/solution.py
@@ -198,7 +198,7 @@
     outgoing_back = jnp.einsum(
         "js,jkxf->skxf", placer, rand_terms, preferred_element_type=jnp.float32
     ).astype(jnp.bfloat16)
-    outgoing_back = outgoing_back.at[0].set(kept.astype(jnp.bfloat16))
+    outgoing_back = jnp.concatenate([kept[None].astype(jnp.bfloat16), outgoing_back[1:]], axis=0)
     arrived = lax.all_to_all(outgoing_back, "seq", split_axis=0, concat_axis=0, tiled=True)
     firsts = arrived.reshape(seq_count, capacity, 2, BLOCK, features)[:, 0]
     firsts = firsts.reshape(seq_count // 2, 2, G, BLOCK, features)

time: 588 us -> 588 us (level)
    scatter x4 -> x0, local copies, waits for them, and re-layouts: 21 us -> none  [attend_chunk(): outgoing_back = outgoing_back.at[0].set(kept.astype(jnp.bfloat16))]
    concatenate x0 -> x2, local copies, waits for them, and re-layouts: none -> 8.95 us  [attend_chunk(): jnp.concatenate([kept[None].astype(jnp.bfloat16), outgoing_back[1:]], axi...]
    unnamed x131 -> x137, local copies, waits for them, and re-layouts: 24.3 us -> 24.6 us
where the time goes in v5:
time: 588 us; the launch traced here: 576 us
  waiting for transfers between devices  215 us (37%)
  local copies, waits for them, and re-layouts  184 us (31%)
  starting transfers between devices  58.8 us (10%)
  other arithmetic  44.6 us (8%)
  blocking collectives  37.5 us (6%)
  matrix products  33.4 us (6%)
    all_to_all x2, waiting for transfers between devices, attend_chunk(): lax.all_to_all(outgoing_back, 'seq', split_axis=0, concat_axis=0, tiled=T...  96 us
    all_to_all x2, waiting for transfers between devices, attend_chunk(): lax.all_to_all(outgoing, 'seq', split_axis=0, concat_axis=0, tiled=True)  84.2 us
    all_to_all x1, blocking collectives, on_device(): lax.all_to_all(result, 'head', split_axis=1, concat_axis=2, tiled=True)  37.5 us
    another operation x10, local copies, waits for them, and re-layouts, attend_chunk(): jnp.stack([key_terms, value_terms]).reshape(2, per_dev, 3, BLOCK, features)  25.3 us
    unnamed x137, local copies, waits for them, and re-layouts  24.6 us
    all_to_all x1, waiting for transfers between devices, on_device(): lax.all_to_all(kv_stacked, 'head', split_axis=2, concat_axis=1, tiled=True)  19.6 us
    all_to_all x2, starting transfers between devices, attend_chunk(): lax.all_to_all(outgoing, 'seq', split_axis=0, concat_axis=0, tiled=True)  15.8 us
    ppermute x7, waiting for transfers between devices, broadcast(): lax.ppermute(block, axis, [(z * inner, z * inner + k) for z in range(oute...  14.7 us
  transfers between devices with their start and end apart: 26, of which 7 were waited for; matrix products, arithmetic and copies ran while one was open for 36% of the time, Pallas kernels for 0%

profile of v5, /device:TPU:8, one launch (start us, length us, event | category | flops | bytes accessed | tf_op | source)
XLA Modules:
  0.0 576.5 jit_solution(925645524547696815)
XLA Ops:
  5.9 4.4 all-to-all-start
  17.0 19.6 %all-to-all-done = bf16[2,160,2048]{1,0,2:T(2,128)(2,1)S(1)} async-done(((bf16[2,160,2048]{1,0,2:T(2,128)(2,1)}), bf16[2,160,2048]{1,0,2:T(2,128)(2,1)S(1)}, u32[]{:S(2)}, u32[]{:S(2)}) %all-to-all-start) | async-done | bytes 1310752 | tf_op jit(solution)/shard_map/all_to_all | solution.py:249
  36.7 4.5 all-to-all-start.1
  66.6 14.7 %collective-permute-done.8 = bf16[2,128,512]{2,1,0:T(8,128)(2,1)S(1)} collective-permute-done((bf16[2,128,512]{2,1,0:T(8,128)(2,1)S(1)}, bf16[2,128,512]{2,1,0:T(8,128)(2,1)S(1)}, u32[]{:S(2)}, u32[]{:S(2)}) %collective-permute-start.8) | collective-permute-done | bytes 262176 | tf_op jit(solution)/shard_map/ppermute | solution.py:27
  84.4 4.5 copy.876
  88.9 9.8 %all-to-all-start.2 = ((bf16[64,2,64,256]{3,2,1,0:T(8,128)(2,1)}), bf16[64,2,64,256]{3,2,1,0:T(8,128)(2,1)}, u32[]{:S(2)}, u32[]{:S(2)}) async-start(bf16[64,2,64,256]{3,2,1,0:T(8,128)(2,1)} %copy.876), calls=%async_computation.2 | async-start | bytes 8388608 | tf_op jit(solution)/shard_map/all_to_all | solution.py:135
  101.6 5.6 copy.986
  122.6 4.5 copy.898
  130.7 63.9 %all-to-all-done.2 = bf16[64,2,64,256]{3,2,1,0:T(8,128)(2,1)} async-done(((bf16[64,2,64,256]{3,2,1,0:T(8,128)(2,1)}), bf16[64,2,64,256]{3,2,1,0:T(8,128)(2,1)}, u32[]{:S(2)}, u32[]{:S(2)}) %all-to-all-start.2) | async-done | bytes 4194336 | tf_op jit(solution)/shard_map/all_to_all | solution.py:135
  194.6 6.1 %all-to-all-start.3 = ((bf16[64,2,64,256]{3,2,1,0:T(8,128)(2,1)}), bf16[64,2,64,256]{3,2,1,0:T(8,128)(2,1)}, u32[]{:S(2)}, u32[]{:S(2)}) async-start(bf16[64,2,64,256]{3,2,1,0:T(8,128)(2,1)} %copy.898), calls=%async_computation.3 | async-start | bytes 8388608 | tf_op jit(solution)/shard_map/all_to_all | solution.py:135
  213.1 4.5 reshape_squeeze.28
  231.3 4.2 gather_fusion.1
  271.9 4.6 copy.935
  276.4 20.3 %all-to-all-done.3 = bf16[64,2,64,256]{3,2,1,0:T(8,128)(2,1)} async-done(((bf16[64,2,64,256]{3,2,1,0:T(8,128)(2,1)}), bf16[64,2,64,256]{3,2,1,0:T(8,128)(2,1)}, u32[]{:S(2)}, u32[]{:S(2)}) %all-to-all-start.3) | async-done | bytes 4194336 | tf_op jit(solution)/shard_map/all_to_all | solution.py:135
  296.7 5.7 all-to-all-start.4
  344.2 4.4 copy.953
  348.6 50.0 %all-to-all-done.4 = bf16[64,2,64,256]{3,2,1,0:T(8,128)(2,1)} async-done(((bf16[64,2,64,256]{3,2,1,0:T(8,128)(2,1)}), bf16[64,2,64,256]{3,2,1,0:T(8,128)(2,1)}, u32[]{:S(2)}, u32[]{:S(2)}) %all-to-all-start.4) | async-done | bytes 4194336 | tf_op jit(solution)/shard_map/all_to_all | solution.py:202
  398.6 6.1 %all-to-all-start.5 = ((bf16[64,2,64,256]{3,2,1,0:T(8,128)(2,1)}), bf16[64,2,64,256]{3,2,1,0:T(8,128)(2,1)}, u32[]{:S(2)}, u32[]{:S(2)}) async-start(bf16[64,2,64,256]{3,2,1,0:T(8,128)(2,1)} %copy.953), calls=%async_computation.5 | async-start | bytes 8388608 | tf_op jit(solution)/shard_map/all_to_all | solution.py:202
  420.2 4.2 reshape.518
  432.6 4.1 reshape.520
  454.7 46.0 %all-to-all-done.5 = bf16[64,2,64,256]{3,2,1,0:T(8,128)(2,1)} async-done(((bf16[64,2,64,256]{3,2,1,0:T(8,128)(2,1)}), bf16[64,2,64,256]{3,2,1,0:T(8,128)(2,1)}, u32[]{:S(2)}, u32[]{:S(2)}) %all-to-all-start.5) | async-done | bytes 4194336 | tf_op jit(solution)/shard_map/all_to_all | solution.py:202
  504.5 4.7 fusion.1
  511.1 5.4 bitcast_add_fusion
  533.5 37.5 %all_to_all.65 = bf16[3,640,512]{2,0,1:T(4,128)(2,1)S(1)} all-to-all(bf16[3,640,512]{2,0,1:T(4,128)(2,1)S(1)} %copy.962), channel_id=1, replica_groups=mesh['seq'=64,'head'=4] {'head'}, dimensions={1} | all-to-all | bytes 3932160 | tf_op jit(solution)/shard_map/all_to_all | solution.py:336
  (377 shorter events, 234.8 us)
Async XLA Ops:
  5.9 30.8 %all-to-all-start = ((bf16[2,160,2048]{1,0,2:T(2,128)(2,1)}), bf16[2,160,2048]{1,0,2:T(2,128)(2,1)S(1)}, u32[]{:S(2)}, u32[]{:S(2)}) async-start(bf16[2,160,2048]{1,0,2:T(2,128)(2,1)} %copy.856), calls=%async_computation | async-start | bytes 4194304 | tf_op jit(solution)/shard_map/all_to_all | solution.py:249
  36.7 52.2 %all-to-all-start.1 = ((bf16[2,160,2048]{1,0,2:T(2,128)(2,1)}), bf16[2,160,2048]{1,0,2:T(2,128)(2,1)}, u32[]{:S(2)}, u32[]{:S(2)}) async-start(bf16[2,160,2048]{1,0,2:T(2,128)(2,1)} %copy.871), calls=%async_computation.1 | async-start | bytes 4194304 | tf_op jit(solution)/shard_map/all_to_all | solution.py:252
  47.4 3.9 collective-permute-start.2
  48.1 5.1 collective-permute-start.3
  48.7 8.1 %collective-permute-start.4 = (bf16[2,128,512]{2,1,0:T(8,128)(2,1)S(1)}, bf16[2,128,512]{2,1,0:T(8,128)(2,1)S(1)}, u32[]{:S(2)}, u32[]{:S(2)}) collective-permute-start(bf16[2,128,512]{2,1,0:T(8,128)(2,1)S(1)} %maximum_select_fusion), channel_id=1, source_target_pairs={{0,160},{1,161},{2,162},{3,163}} | collective-permute-start | bytes 786440 | tf_op jit(solution)/shard_map/ppermute | solution.py:22
  49.5 7.4 %collective-permute-start.5 = (bf16[2,128,512]{2,1,0:T(8,128)(2,1)S(1)}, bf16[2,128,512]{2,1,0:T(8,128)(2,1)S(1)}, u32[]{:S(2)}, u32[]{:S(2)}) collective-permute-start(bf16[2,128,512]{2,1,0:T(8,128)(2,1)S(1)} %maximum_select_fusion), channel_id=1, source_target_pairs={{0,192},{1,193},{2,194},{3,195}} | collective-permute-start | bytes 786440 | tf_op jit(solution)/shard_map/ppermute | solution.py:22
  50.2 6.7 %collective-permute-start.6 = (bf16[2,128,512]{2,1,0:T(8,128)(2,1)S(1)}, bf16[2,128,512]{2,1,0:T(8,128)(2,1)S(1)}, u32[]{:S(2)}, u32[]{:S(2)}) collective-permute-start(bf16[2,128,512]{2,1,0:T(8,128)(2,1)S(1)} %maximum_select_fusion), channel_id=1, source_target_pairs={{0,224},{1,225},{2,226},{3,227}} | collective-permute-start | bytes 786440 | tf_op jit(solution)/shard_map/ppermute | solution.py:22
  51.3 8.2 %collective-permute-start.14 = (bf16[2,64,512]{2,1,0:T(8,128)(2,1)S(1)}, bf16[2,64,512]{2,1,0:T(8,128)(2,1)S(1)}, u32[]{:S(2)}, u32[]{:S(2)}) collective-permute-start(bf16[2,64,512]{2,1,0:T(8,128)(2,1)S(1)} %get-tuple-element.75), channel_id=1, source_target_pairs={{0,4},{4,8},{8,12},{12,16},{16,20},{20,24},{24,28},{28,32},{32,36}... | collective-permute-start | bytes 393224 | tf_op jit(solution)/shard_map/ppermute | solution.py:67
  53.2 7.0 %collective-permute-start.15 = (bf16[2,64,512]{2,1,0:T(8,128)(2,1)S(1)}, bf16[2,64,512]{2,1,0:T(8,128)(2,1)S(1)}, u32[]{:S(2)}, u32[]{:S(2)}) collective-permute-start(bf16[2,64,512]{2,1,0:T(8,128)(2,1)S(1)} %get-tuple-element.76), channel_id=1, source_target_pairs={{4,0},{8,4},{12,8},{16,12},{20,16},{24,20},{28,24},{32,28},{36,32}... | collective-permute-start | bytes 393224 | tf_op jit(solution)/shard_map/ppermute | solution.py:68
  57.0 3.9 collective-permute-start.10
  57.7 4.5 collective-permute-start.11
  58.8 7.7 %collective-permute-start.12 = (bf16[2,128,512]{2,1,0:T(8,128)(2,1)S(1)}, bf16[2,128,512]{2,1,0:T(8,128)(2,1)S(1)}, u32[]{:S(2)}, u32[]{:S(2)}) collective-permute-start(bf16[2,128,512]{2,1,0:T(8,128)(2,1)S(1)} %add_add_fusion.1), channel_id=1, source_target_pairs={{0,24},{32,56},{64,88},{96,120},{128,152},{160,184},{192,216},{224... | collective-permute-start | bytes 786440 | tf_op jit(solution)/shard_map/ppermute | solution.py:27
  59.5 7.0 %collective-permute-start.13 = (bf16[2,128,512]{2,1,0:T(8,128)(2,1)S(1)}, bf16[2,128,512]{2,1,0:T(8,128)(2,1)S(1)}, u32[]{:S(2)}, u32[]{:S(2)}) collective-permute-start(bf16[2,128,512]{2,1,0:T(8,128)(2,1)S(1)} %add_add_fusion.1), channel_id=1, source_target_pairs={{0,28},{32,60},{64,92},{96,124},{128,156},{160,188},{192,220},{224... | collective-permute-start | bytes 786440 | tf_op jit(solution)/shard_map/ppermute | solution.py:27
  60.2 6.3 %collective-permute-start.7 = (bf16[2,128,512]{2,1,0:T(8,128)(2,1)S(1)}, bf16[2,128,512]{2,1,0:T(8,128)(2,1)S(1)}, u32[]{:S(2)}, u32[]{:S(2)}) collective-permute-start(bf16[2,128,512]{2,1,0:T(8,128)(2,1)S(1)} %add_add_fusion.1), channel_id=1, source_target_pairs={{0,4},{32,36},{64,68},{96,100},{128,132},{160,164},{192,196},{224,... | collective-permute-start | bytes 786440 | tf_op jit(solution)/shard_map/ppermute | solution.py:27
  60.9 20.3 %collective-permute-start.8 = (bf16[2,128,512]{2,1,0:T(8,128)(2,1)S(1)}, bf16[2,128,512]{2,1,0:T(8,128)(2,1)S(1)}, u32[]{:S(2)}, u32[]{:S(2)}) collective-permute-start(bf16[2,128,512]{2,1,0:T(8,128)(2,1)S(1)} %add_add_fusion.1), channel_id=1, source_target_pairs={{0,8},{32,40},{64,72},{96,104},{128,136},{160,168},{192,200},{224,... | collective-permute-start | bytes 786440 | tf_op jit(solution)/shard_map/ppermute | solution.py:27
  62.2 19.0 %collective-permute-start.9 = (bf16[2,128,512]{2,1,0:T(8,128)(2,1)S(1)}, bf16[2,128,512]{2,1,0:T(8,128)(2,1)S(1)}, u32[]{:S(2)}, u32[]{:S(2)}) collective-permute-start(bf16[2,128,512]{2,1,0:T(8,128)(2,1)S(1)} %add_add_fusion.1), channel_id=1, source_target_pairs={{0,12},{32,44},{64,76},{96,108},{128,140},{160,172},{192,204},{224... | collective-permute-start | bytes 786440 | tf_op jit(solution)/shard_map/ppermute | solution.py:27
  88.9 105.7 %all-to-all-start.2 = ((bf16[64,2,64,256]{3,2,1,0:T(8,128)(2,1)}), bf16[64,2,64,256]{3,2,1,0:T(8,128)(2,1)}, u32[]{:S(2)}, u32[]{:S(2)}) async-start(bf16[64,2,64,256]{3,2,1,0:T(8,128)(2,1)} %copy.876), calls=%async_computation.2 | async-start | bytes 8388608 | tf_op jit(solution)/shard_map/all_to_all | solution.py:135
  194.6 102.1 %all-to-all-start.3 = ((bf16[64,2,64,256]{3,2,1,0:T(8,128)(2,1)}), bf16[64,2,64,256]{3,2,1,0:T(8,128)(2,1)}, u32[]{:S(2)}, u32[]{:S(2)}) async-start(bf16[64,2,64,256]{3,2,1,0:T(8,128)(2,1)} %copy.898), calls=%async_computation.3 | async-start | bytes 8388608 | tf_op jit(solution)/shard_map/all_to_all | solution.py:135
  257.9 10.2 %collective-permute-start.16 = (f32[2,64,256]{2,1,0:T(8,128)}, f32[2,64,256]{2,1,0:T(8,128)}, u32[]{:S(2)}, u32[]{:S(2)}) collective-permute-start(f32[2,64,256]{2,1,0:T(8,128)} %bitcast.346), channel_id=1, source_target_pairs={{0,4},{4,0},{8,12},{12,8},{16,20},{20,16},{24,28},{28,24},{32,36},... | collective-permute-start | bytes 393224 | tf_op jit(solution)/shard_map/ppermute | solution.py:194
  296.7 101.9 %all-to-all-start.4 = ((bf16[64,2,64,256]{3,2,1,0:T(8,128)(2,1)}), bf16[64,2,64,256]{3,2,1,0:T(8,128)(2,1)}, u32[]{:S(2)}, u32[]{:S(2)}) async-start(bf16[64,2,64,256]{3,2,1,0:T(8,128)(2,1)} %copy.935), calls=%async_computation.4 | async-start | bytes 8388608 | tf_op jit(solution)/shard_map/all_to_all | solution.py:202
  324.5 16.9 %collective-permute-start.17 = (f32[2,64,256]{2,1,0:T(8,128)S(1)}, f32[2,64,256]{2,1,0:T(8,128)S(1)}, u32[]{:S(2)}, u32[]{:S(2)}) collective-permute-start(f32[2,64,256]{2,1,0:T(8,128)S(1)} %bitcast.423), channel_id=1, source_target_pairs={{0,4},{4,0},{8,12},{12,8},{16,20},{20,16},{24,28},{28,24},{32,36},... | collective-permute-start | bytes 393224 | tf_op jit(solution)/shard_map/ppermute | solution.py:194
  398.6 102.1 %all-to-all-start.5 = ((bf16[64,2,64,256]{3,2,1,0:T(8,128)(2,1)}), bf16[64,2,64,256]{3,2,1,0:T(8,128)(2,1)}, u32[]{:S(2)}, u32[]{:S(2)}) async-start(bf16[64,2,64,256]{3,2,1,0:T(8,128)(2,1)} %copy.953), calls=%async_computation.5 | async-start | bytes 8388608 | tf_op jit(solution)/shard_map/all_to_all | solution.py:202
  519.0 7.4 %collective-permute-start.18 = (bf16[2,64,512]{2,1,0:T(8,128)(2,1)S(1)}, bf16[2,64,512]{2,1,0:T(8,128)(2,1)S(1)}, u32[]{:S(2)}, u32[]{:S(2)}) collective-permute-start(bf16[2,64,512]{2,1,0:T(8,128)(2,1)S(1)} %get-tuple-element.89), channel_id=1, source_target_pairs={{0,4},{4,8},{8,12},{12,16},{16,20},{20,24},{24,28},{28,32},{32,36}... | collective-permute-start | bytes 393224 | tf_op jit(solution)/shard_map/ppermute | solution.py:67
  521.1 6.1 %collective-permute-start.19 = (bf16[2,64,512]{2,1,0:T(8,128)(2,1)S(1)}, bf16[2,64,512]{2,1,0:T(8,128)(2,1)S(1)}, u32[]{:S(2)}, u32[]{:S(2)}) collective-permute-start(bf16[2,64,512]{2,1,0:T(8,128)(2,1)S(1)} %get-tuple-element.90), channel_id=1, source_target_pairs={{4,0},{8,4},{12,8},{16,12},{20,16},{24,20},{28,24},{32,28},{36,32}... | collective-permute-start | bytes 393224 | tf_op jit(solution)/shard_map/ppermute | solution.py:68
  (67 other events, 191.3 us)
